TPU v7x, 256 devices: a whole 4x4x8 slice. The times are simulated.
256 devices in a mesh: row: 64 (over z_hi, y, x), col: 4 (over z_lo, core).
Axes of the slice: x: 4, y: 4, z: 8 (z_hi: 4, z_lo: 2; z = z_hi * 2 + z_lo), core: 2. Of those that a mesh axis runs over, the one named last changes fastest.
Arguments:
- amplitudes: float32 [6400, 12800], P('row', 'col'), may hold values from -6 to 6
- intermediate: float32 [1600, 8192], P('row', 'col'), may hold values from -0.15625 to 0.15625
Outputs:
- cycle_term: float32 [51200, 8192], P('row', 'col')
All inputs are finite; a program needn't handle non-finite values.
Results may differ from a plain program's by a relative error of at most 0.00007.
Values sent between devices are 32-bit elements; how exact they have to be, the bound alone decides.
No kernel may reach another device: no remote copies, remote signals or barrier semaphores. Data moves between devices by JAX's collectives and lax.ppermute only.
A program may use at most 128 MiB of HBM per device.

v0:
```python
import jax
import jax.numpy as jnp
from jax import lax
from jax.sharding import Mesh, PartitionSpec as P

O = 40
V = 320
ROW = ("zh", "y", "x")
COL = ("zl", "core")
CHUNKS = 2


def regroup_local(amplitudes, row_count):
    pair_rows = amplitudes.shape[0]
    b_count = amplitudes.shape[1] // V
    virt_local = V // row_count
    outgoing = amplitudes.reshape(pair_rows, b_count, V).transpose(2, 1, 0)
    received = lax.all_to_all(outgoing, ROW, split_axis=0, concat_axis=2, tiled=True)
    set_rows = received.shape[2] // O
    blocks = received.reshape(virt_local, b_count, set_rows, O).transpose(0, 2, 1, 3)
    return blocks.reshape(virt_local * set_rows, b_count * O)


def ring_zh(part):
    right = [(i, (i + 1) % 4) for i in range(4)]
    left = [(i, (i - 1) % 4) for i in range(4)]
    from_left = lax.ppermute(part, "zh", right)
    from_right = lax.ppermute(part, "zh", left)
    from_far = lax.ppermute(from_left, "zh", right)
    return jnp.concatenate([part, from_right, from_far, from_left], axis=0)


def exchange_col(block, slots):
    zl = lax.axis_index("zl")
    core = lax.axis_index("core")
    zh = lax.axis_index("zh")
    me = zl * 2 + core
    from_zl = lax.ppermute(block, "zl", [(0, 1), (1, 0)])
    pair = jnp.stack([block, from_zl])
    from_core = lax.ppermute(pair, "core", [(0, 1), (1, 0)])
    by_d = (block, from_core[0], from_zl, from_core[1])
    rows, width = block.shape
    outs = []
    for s in range(4):
        d = jnp.bitwise_xor(me, lax.rem(s + zh, 4))
        pick = jnp.where(d == 0, by_d[0], jnp.where(d == 1, by_d[1], jnp.where(d == 2, by_d[2], by_d[3])))
        outs.append(pick.reshape(rows, slots[0], 1, slots[1]))
    return jnp.concatenate(outs, axis=2).reshape(rows, 4 * width)


def local(amplitudes, intermediate):
    row_count = 64
    block = regroup_local(amplitudes, row_count)
    yx = 16
    piece = intermediate.shape[0]
    regrouped = exchange_col(block, (yx, piece))
    ringed = ring_zh(intermediate)
    cols = intermediate.shape[1]
    step = cols // CHUNKS
    outs = []
    for c in range(CHUNKS):
        part = ringed[:, c * step:(c + 1) * step]
        part = lax.all_gather(part, ("y", "x"), axis=0, tiled=True)
        outs.append(
            jnp.dot(regrouped, part, precision=lax.Precision.HIGH, preferred_element_type=jnp.float32)
        )
    return jnp.concatenate(outs, axis=1)


def solution(mesh):
    devices = mesh.devices.reshape(4, 4, 4, 2, 2)
    fine = Mesh(devices, ROW + COL)
    spec = P(ROW, COL)
    return jax.shard_map(local, mesh=fine, in_specs=(spec, spec), out_specs=spec, check_vma=False)
```

profile of v0, /device:TPU:1, one launch (start us, length us, event | category | flops | bytes accessed | tf_op | source)
XLA Modules:
  0.0 240.0 jit_solution(13974046641622552710)
XLA Ops:
  6.5 0.0 copy-start.2
  6.5 0.0 all-gather.5.cloned.1.call-start
  6.5 3.8 %collective-permute-start.3 = (f32[25,2048]{1,0:T(8,128)}, f32[25,2048]{1,0:T(8,128)S(1)}, u32[]{:S(2)}, u32[]{:S(2)}) collective-permute-start(f32[25,2048]{1,0:T(8,128)} %param.3), channel_id=1, source_target_pairs={{0,64},{64,128},{128,192},{192,0},{1,65},{65,129},{129,193},{193,1... | collective-permute-start | bytes 614408 | tf_op jit(solution)/shard_map/ppermute | solution.py:27
  10.3 3.0 %collective-permute-start.2 = (f32[25,2048]{1,0:T(8,128)}, f32[25,2048]{1,0:T(8,128)S(1)}, u32[]{:S(2)}, u32[]{:S(2)}) collective-permute-start(f32[25,2048]{1,0:T(8,128)} %param.3), channel_id=1, source_target_pairs={{0,192},{64,0},{128,64},{192,128},{1,193},{65,1},{129,65},{193,129... | collective-permute-start | bytes 614408 | tf_op jit(solution)/shard_map/ppermute | solution.py:28
  13.4 7.8 %collective-permute-done.3 = f32[25,2048]{1,0:T(8,128)S(1)} collective-permute-done((f32[25,2048]{1,0:T(8,128)}, f32[25,2048]{1,0:T(8,128)S(1)}, u32[]{:S(2)}, u32[]{:S(2)}) %collective-permute-start.3) | collective-permute-done | bytes 204832 | tf_op jit(solution)/shard_map/ppermute | solution.py:27
  21.2 4.8 %collective-permute-start.4 = (f32[25,2048]{1,0:T(8,128)S(1)}, f32[25,2048]{1,0:T(8,128)S(1)}, u32[]{:S(2)}, u32[]{:S(2)}) collective-permute-start(f32[25,2048]{1,0:T(8,128)S(1)} %collective-permute-done.3), channel_id=1, source_target_pairs={{0,64},{64,128},{128,192},{192,0},{1,65},{65,129},{129,193},{193,1... | collective-permute-start | bytes 614408 | tf_op jit(solution)/shard_map/ppermute | solution.py:29
  26.0 0.8 collective-permute-done.2
  26.7 7.5 %collective-permute-done.4 = f32[25,2048]{1,0:T(8,128)S(1)} collective-permute-done((f32[25,2048]{1,0:T(8,128)S(1)}, f32[25,2048]{1,0:T(8,128)S(1)}, u32[]{:S(2)}, u32[]{:S(2)}) %collective-permute-start.4) | collective-permute-done | bytes 204832 | tf_op jit(solution)/shard_map/ppermute | solution.py:29
  34.2 1.0 pad_maximum_fusion.3
  35.3 1.0 slice_bitcast_fusion.3
  36.3 0.0 all-gather.5.cloned.1.call-update
  36.3 0.0 all-gather.7.cloned.1.call-start
  36.4 0.7 all-gather.7.cloned.1.call-update
  37.1 0.0 copy-done.2
  37.1 1.7 copy.8
  38.8 2.4 %copy.9 = f32[320,10,100]{2,1,0:T(8,128)S(1)} copy(f32[320,10,100]{2,0,1:T(8,128)} %bitcast.55) | data formatting | bytes 2560000 | tf_op jit(solution)/shard_map/transpose | solution.py:17
  41.2 4.1 %reshape.37 = f32[64,1,5000]{2,1,0:T(1,128)} reshape(f32[320,10,100]{2,1,0:T(8,128)S(1)} %copy.9) | data formatting | bytes 2560000
  45.3 49.0 %all_to_all.15 = f32[64,1,5000]{2,1,0:T(1,128)S(1)} all-to-all(f32[64,1,5000]{2,1,0:T(1,128)} %reshape.37), channel_id=1, replica_groups=mesh['zh'=4,'y'=4,'x'=4,'zl'=2,'core'=2] {'zh','y','x'}, dimensions={0} | all-to-all | bytes 2560000 | tf_op jit(solution)/shard_map/all_to_all | solution.py:18
  94.3 0.5 broadcast.4
  94.8 5.0 %reduce = f32[64,5000]{1,0:T(8,128)} reduce(f32[64,1,5000]{2,1,0:T(1,128)S(1)} %all_to_all.15, f32[]{:T(128)} %broadcast.4), dimensions={1}, to_apply=%all_to_all.11.reduce_sub_computation | reduce | bytes 2560004 | tf_op jit(solution)/shard_map/all_to_all | solution.py:18
  99.8 2.6 %reshape.38 = f32[320,10,100]{2,1,0:T(8,128)S(1)} reshape(f32[64,5000]{1,0:T(8,128)} %reduce) | data formatting | bytes 2560000
  102.4 1.7 copy.11
  104.1 4.7 %reshape.26 = f32[5,10,160,40]{3,2,1,0:T(8,128)} reshape(f32[5,10,64,100]{3,2,1,0:T(8,128)} %copy.11) | data formatting | bytes 2560000 | tf_op jit(solution)/shard_map/reshape | solution.py:20
  108.8 5.2 %copy.12 = f32[5,160,10,40]{1,0,3,2:T(8,128)S(1)} copy(f32[5,160,10,40]{3,1,2,0:T(8,128)} %bitcast.53) | data formatting | bytes 2560000 | tf_op jit(solution)/shard_map/transpose | solution.py:20
  114.1 1.8 reshape.27
  115.9 0.0 collective-permute-start
  115.9 1.8 stack_reshape.3
  117.7 30.7 %collective-permute-done = f32[800,400]{0,1:T(8,128)} collective-permute-done((f32[800,400]{0,1:T(8,128)}, f32[800,400]{0,1:T(8,128)}, u32[]{:S(2)}, u32[]{:S(2)}) %collective-permute-start) | collective-permute-done | bytes 1280032 | tf_op jit(solution)/shard_map/ppermute | solution.py:38
  148.5 3.7 %pad_maximum_fusion.2 = f32[2,800,400]{1,2,0:T(8,128)} fusion(f32[1,800,400]{1,2,0:T(8,128)} %bitcast.6, f32[1,800,400]{1,2,0:T(8,128)} %stack_reshape.3), kind=kLoop, calls=%fused_computation.2 | loop fusion | flops 640000 | bytes 5120000 | tf_op jit(solution)/shard_map/stack | solution.py:39
  152.1 1.6 collective-permute-start.1
  153.8 5.2 %collective-permute-done.1 = f32[2,800,400]{1,2,0:T(8,128)} collective-permute-done((f32[2,800,400]{1,2,0:T(8,128)}, f32[2,800,400]{1,2,0:T(8,128)}, u32[]{:S(2)}, u32[]{:S(2)}) %collective-permute-start.1) | collective-permute-done | bytes 2560032 | tf_op jit(solution)/shard_map/ppermute | solution.py:40
  159.0 0.0 copy-done
  159.0 3.1 %select_select_fusion.2 = f32[800,400]{0,1:T(8,128)} fusion(f32[800,400]{0,1:T(8,128)S(1)} %copy-done, f32[800,400]{0,1:T(8,128)} %collective-permute-done, f32[2,800,400]{1,2,0:T(8,128)} %collective-permute-done.1, pred[]{:T(512)S(6)} %eq.41, pred[]{:T(512)S(6)} %eq.40, pred[]{:T(512)S(6)} %eq.39), kind=kLoop, calls=%fused_computation.7 | loop fusion | flops 960000 | bytes 6400003 | tf_op jit(solution)/shard_map/jit(_where)/select_n | solution.py:46
  162.1 1.7 reshape.29
  163.8 4.6 %select_select_fusion.3 = (f32[800,400]{0,1:T(8,128)}, f32[800,400]{0,1:T(8,128)}, f32[800,400]{0,1:T(8,128)}) fusion(f32[800,400]{0,1:T(8,128)S(1)} %copy-done, f32[800,400]{0,1:T(8,128)} %collective-permute-done, f32[2,800,400]{1,2,0:T(8,128)} %collective-permute-done.1, pred[]{:T(512)S(6)} %eq.38, pred[]{:T(512)S(6)} %eq.37, pred[]{:T(512)S(6)} %eq.36, ...), kind=kLoop, calls=%fused_computation.8 | loop fusion | flops 2880000 | bytes 8960009 | tf_op jit(solution)/shard_map/jit(_where)/select_n | solution.py:46
  168.4 3.0 %reshape.28 = f32[800,16,1,25]{0,3,1,2:T(8,128)} reshape(f32[800,400]{0,1:T(8,128)} %get-tuple-element.5) | data formatting | bytes 2560000 | tf_op jit(solution)/shard_map/reshape | solution.py:47
  171.3 2.9 %reshape.30 = f32[800,16,1,25]{0,3,1,2:T(8,128)} reshape(f32[800,400]{0,1:T(8,128)} %get-tuple-element.7) | data formatting | bytes 2560000 | tf_op jit(solution)/shard_map/reshape | solution.py:47
  174.2 0.0 copy-done.1
  174.2 1.4 reshape.31
  175.6 3.0 %pad_maximum_fusion = f32[800,16,4,25]{0,3,1,2:T(8,128)S(1)} fusion(f32[800,16,1,25]{0,3,1,2:T(8,128)} %reshape.31, f32[800,16,1,25]{0,3,1,2:T(8,128)} %reshape.30, f32[800,16,1,25]{0,3,1,2:T(8,128)S(1)} %reshape.29, f32[800,16,1,25]{0,3,1,2:T(8,128)} %reshape.28), kind=kLoop, calls=%fused_computation | loop fusion | flops 3840000 | bytes 10240000 | tf_op jit(solution)/shard_map/concatenate | solution.py:48
  178.7 3.6 %copy.14 = f32[800,16,4,25]{0,3,2,1:T(8,128)} copy(f32[800,16,4,25]{0,3,1,2:T(8,128)S(1)} %pad_maximum_fusion) | data formatting | bytes 10240000 | tf_op jit(solution)/shard_map/concatenate | solution.py:48
  182.3 6.2 %reshape.32 = f32[800,1600]{0,1:T(8,128)} reshape(f32[800,16,4,25]{0,3,2,1:T(8,128)} %copy.14) | data formatting | bytes 10240000 | tf_op jit(solution)/shard_map/reshape | solution.py:48
  188.5 6.2 %reshape.34 = f32[1600,1024]{1,0:T(8,128)} reshape(f32[16,100,1024]{2,1,0:T(8,128)} %all-gather.5.cloned.1.call-done) | data formatting | bytes 13107200
  194.7 14.3 %fusion = f32[800,1024]{1,0:T(8,128)S(1)} fusion(f32[800,1600]{0,1:T(8,128)} %reshape.32, f32[1600,1024]{1,0:T(8,128)} %reshape.34), kind=kOutput, calls=%fused_computation.12 | convolution fusion | flops 7864320000 | bytes 14950400 | tf_op jit(solution)/shard_map/dot_general | solution.py:65
  209.0 0.0 all-gather.7.cloned.1.call-done
  209.1 6.2 %reshape.36 = f32[1600,1024]{1,0:T(8,128)} reshape(f32[16,100,1024]{2,1,0:T(8,128)} %all-gather.7.cloned.1.call-done) | data formatting | bytes 13107200
  215.3 14.5 %fusion.1 = f32[800,1024]{1,0:T(8,128)S(1)} fusion(f32[800,1600]{0,1:T(8,128)} %reshape.32, f32[1600,1024]{1,0:T(8,128)} %reshape.36), kind=kOutput, calls=%fused_computation.13 | convolution fusion | flops 7864320000 | bytes 14950400 | tf_op jit(solution)/shard_map/dot_general | solution.py:65
  229.7 3.4 %pad_maximum_fusion.1 = f32[800,2048]{1,0:T(8,128)} fusion(f32[800,1024]{1,0:T(8,128)S(1)} %fusion.1, f32[800,1024]{1,0:T(8,128)S(1)} %fusion), kind=kLoop, calls=%fused_computation.1 | loop fusion | flops 1638400 | bytes 13107200 | tf_op jit(solution)/shard_map/concatenate | solution.py:67
  (3 shorter events, 0.0 us)
Async XLA Ops:
  6.5 30.6 %copy-start.2 = (f32[100,3200]{1,0:T(8,128)S(1)}, f32[100,3200]{1,0:T(8,128)}, u32[]{:S(2)}) copy-start(f32[100,3200]{1,0:T(8,128)} %param.2) | copy-start | bytes 3840004
  6.5 182.0 %all-gather.5.cloned.1.call-start = ((), (), s32[]{:S(2)}) async-start(), calls=%async_computation.1 | async-start | bytes 7241728 | tf_op jit(solution)/shard_map/all_gather | solution.py:63
  6.5 14.6 %collective-permute-start.3 = (f32[25,2048]{1,0:T(8,128)}, f32[25,2048]{1,0:T(8,128)S(1)}, u32[]{:S(2)}, u32[]{:S(2)}) collective-permute-start(f32[25,2048]{1,0:T(8,128)} %param.3), channel_id=1, source_target_pairs={{0,64},{64,128},{128,192},{192,0},{1,65},{65,129},{129,193},{193,1... | collective-permute-start | bytes 614408 | tf_op jit(solution)/shard_map/ppermute | solution.py:27
  10.3 16.4 %collective-permute-start.2 = (f32[25,2048]{1,0:T(8,128)}, f32[25,2048]{1,0:T(8,128)S(1)}, u32[]{:S(2)}, u32[]{:S(2)}) collective-permute-start(f32[25,2048]{1,0:T(8,128)} %param.3), channel_id=1, source_target_pairs={{0,192},{64,0},{128,64},{192,128},{1,193},{65,1},{129,65},{193,129... | collective-permute-start | bytes 614408 | tf_op jit(solution)/shard_map/ppermute | solution.py:28
  21.2 13.1 %collective-permute-start.4 = (f32[25,2048]{1,0:T(8,128)S(1)}, f32[25,2048]{1,0:T(8,128)S(1)}, u32[]{:S(2)}, u32[]{:S(2)}) collective-permute-start(f32[25,2048]{1,0:T(8,128)S(1)} %collective-permute-done.3), channel_id=1, source_target_pairs={{0,64},{64,128},{128,192},{192,0},{1,65},{65,129},{129,193},{193,1... | collective-permute-start | bytes 614408 | tf_op jit(solution)/shard_map/ppermute | solution.py:29
  36.3 172.7 %all-gather.7.cloned.1.call-start = ((), (), s32[]{:S(2)}) async-start(), calls=%async_computation.2 | async-start | bytes 7241728 | tf_op jit(solution)/shard_map/all_gather | solution.py:63
  115.9 32.5 %collective-permute-start = (f32[800,400]{0,1:T(8,128)}, f32[800,400]{0,1:T(8,128)}, u32[]{:S(2)}, u32[]{:S(2)}) collective-permute-start(f32[800,400]{0,1:T(8,128)} %reshape.27), channel_id=1, source_target_pairs={{0,2},{2,0},{1,3},{3,1},{4,6},{6,4},{5,7},{7,5},{8,10},{10,8},{9,1... | collective-permute-start | bytes 3840008 | tf_op jit(solution)/shard_map/ppermute | solution.py:38
  148.5 10.5 %copy-start = (f32[800,400]{0,1:T(8,128)S(1)}, f32[800,400]{0,1:T(8,128)}, u32[]{:S(2)}) copy-start(f32[800,400]{0,1:T(8,128)} %reshape.27) | copy-start | bytes 3840004
  152.1 6.8 %collective-permute-start.1 = (f32[2,800,400]{1,2,0:T(8,128)}, f32[2,800,400]{1,2,0:T(8,128)}, u32[]{:S(2)}, u32[]{:S(2)}) collective-permute-start(f32[2,800,400]{1,2,0:T(8,128)} %pad_maximum_fusion.2), channel_id=1, source_target_pairs={{0,1},{1,0},{2,3},{3,2},{4,5},{5,4},{6,7},{7,6},{8,9},{9,8},{10,11... | collective-permute-start | bytes 7680008 | tf_op jit(solution)/shard_map/ppermute | solution.py:40
  168.4 5.8 %copy-start.1 = (f32[800,400]{0,1:T(8,128)S(1)}, f32[800,400]{0,1:T(8,128)}, u32[]{:S(2)}) copy-start(f32[800,400]{0,1:T(8,128)} %get-tuple-element.6) | copy-start | bytes 3840004
Sparse Core Ops, SparseCore 0:
  36.5 86.3 all-gather.4
  125.3 68.4 all-gather.6
where the time goes:
time: 241 us; the launch traced here: 240 us
  local copies, waits for them, and re-layouts  58.8 us (24%)
  waiting for transfers between devices  52.7 us (22%)
  blocking collectives  49 us (20%)
  matrix products  28.8 us (12%)
  other arithmetic  23.9 us (10%)
  between operations  13.5 us (6%)
  starting transfers between devices  13.3 us (6%)
    all_to_all x1, blocking collectives, regroup_local(): lax.all_to_all(outgoing, ROW, split_axis=0, concat_axis=2, tiled=True)  49 us
    ppermute x1, waiting for transfers between devices, exchange_col(): from_zl = lax.ppermute(block, 'zl', [(0, 1), (1, 0)])  30.7 us
    dot_general x2, matrix products, local(): jnp.dot(regrouped, part, precision=lax.Precision.HIGH, preferred_element_...  28.8 us
    unnamed x12, local copies, waits for them, and re-layouts  21.8 us
    reshape x4, local copies, waits for them, and re-layouts, exchange_col(): outs.append(pick.reshape(rows, slots[0], 1, slots[1]))  8.9 us
    ppermute x1, waiting for transfers between devices, ring_zh(): from_left = lax.ppermute(part, 'zh', right)  7.77 us
    select_n x2, other arithmetic, exchange_col(): jnp.where(d == 0, by_d[0], jnp.where(d == 1, by_d[1], jnp.where(d == 2, b...  7.74 us
    ppermute x1, waiting for transfers between devices, ring_zh(): from_far = lax.ppermute(from_left, 'zh', right)  7.52 us
  transfers between devices with their start and end apart: 7, of which 5 were waited for; matrix products, arithmetic and copies ran while one was open for 36% of the time, Pallas kernels for 0%

commit v1 on v0

--- a/solution.py
+++ b/solution.py
@@ -7,7 +7,7 @@
 V = 320
 ROW = ("zh", "y", "x")
 COL = ("zl", "core")
-CHUNKS = 2
+CHUNKS = 1
 
 
 def regroup_local(amplitudes, row_count):
@@ -53,8 +53,8 @@
     block = regroup_local(amplitudes, row_count)
     yx = 16
     piece = intermediate.shape[0]
+    ringed = ring_zh(intermediate)
     regrouped = exchange_col(block, (yx, piece))
-    ringed = ring_zh(intermediate)
     cols = intermediate.shape[1]
     step = cols // CHUNKS
     outs = []

time: 241 us -> 232 us (0.963)
  matrix products: 28.8 us -> 25.7 us
  other arithmetic: 23.9 us -> 21.4 us
    concatenate x2 -> x0, other arithmetic: 4.47 us -> none  [the longest x1 3.42 us: local(): return jnp.concatenate(outs, axis=1)]
    dot_general x2 -> x1, matrix products: 28.8 us -> 25.7 us  [local(): jnp.dot(regrouped, part, precision=lax.Precision.HIGH, preferred_element_...]
    unnamed x12 -> x10, local copies, waits for them, and re-layouts: 21.8 us -> 20.5 us
  transfers between devices with their start and end apart: 7 -> 6, of which waited for: 5 -> 5; matrix products, arithmetic and copies ran while one was open for 36% -> 28% of each run, Pallas kernels for 0% -> 0%
where the time goes in v1:
time: 232 us
  local copies, waits for them, and re-layouts  57 us (25%)
  waiting for transfers between devices  52 us (22%)
  blocking collectives  49 us (21%)
  matrix products  25.7 us (11%)
  other arithmetic  21.4 us (9%)
  between operations  13.4 us (6%)
  starting transfers between devices  13.3 us (6%)
    all_to_all x1, blocking collectives, regroup_local(): lax.all_to_all(outgoing, ROW, split_axis=0, concat_axis=2, tiled=True)  49 us
    ppermute x1, waiting for transfers between devices, exchange_col(): from_zl = lax.ppermute(block, 'zl', [(0, 1), (1, 0)])  30.7 us
    dot_general x1, matrix products, local(): jnp.dot(regrouped, part, precision=lax.Precision.HIGH, preferred_element_...  25.7 us
    unnamed x10, local copies, waits for them, and re-layouts  20.5 us
    reshape x4, local copies, waits for them, and re-layouts, exchange_col(): outs.append(pick.reshape(rows, slots[0], 1, slots[1]))  8.62 us
    ppermute x1, waiting for transfers between devices, ring_zh(): from_left = lax.ppermute(part, 'zh', right)  7.77 us
    select_n x2, other arithmetic, exchange_col(): jnp.where(d == 0, by_d[0], jnp.where(d == 1, by_d[1], jnp.where(d == 2, b...  7.7 us
    ppermute x1, waiting for transfers between devices, ring_zh(): from_far = lax.ppermute(from_left, 'zh', right)  7.52 us
  transfers between devices with their start and end apart: 6, of which 5 were waited for; matrix products, arithmetic and copies ran while one was open for 28% of the time, Pallas kernels for 0%

profile of v1, /device:TPU:1, one launch (start us, length us, event | category | flops | bytes accessed | tf_op | source)
XLA Modules:
  0.0 231.8 jit_solution(3746760943587271116)
XLA Ops:
  6.5 0.0 copy-start.2
  6.5 0.0 all-gather.3.cloned.1.call-start
  6.5 3.8 %collective-permute-start.3 = (f32[25,2048]{1,0:T(8,128)}, f32[25,2048]{1,0:T(8,128)S(1)}, u32[]{:S(2)}, u32[]{:S(2)}) collective-permute-start(f32[25,2048]{1,0:T(8,128)} %param.3), channel_id=1, source_target_pairs={{0,64},{64,128},{128,192},{192,0},{1,65},{65,129},{129,193},{193,1... | collective-permute-start | bytes 614408 | tf_op jit(solution)/shard_map/ppermute | solution.py:27
  10.3 3.0 %collective-permute-start.2 = (f32[25,2048]{1,0:T(8,128)}, f32[25,2048]{1,0:T(8,128)S(1)}, u32[]{:S(2)}, u32[]{:S(2)}) collective-permute-start(f32[25,2048]{1,0:T(8,128)} %param.3), channel_id=1, source_target_pairs={{0,192},{64,0},{128,64},{192,128},{1,193},{65,1},{129,65},{193,129... | collective-permute-start | bytes 614408 | tf_op jit(solution)/shard_map/ppermute | solution.py:28
  13.4 7.8 %collective-permute-done.3 = f32[25,2048]{1,0:T(8,128)S(1)} collective-permute-done((f32[25,2048]{1,0:T(8,128)}, f32[25,2048]{1,0:T(8,128)S(1)}, u32[]{:S(2)}, u32[]{:S(2)}) %collective-permute-start.3) | collective-permute-done | bytes 204832 | tf_op jit(solution)/shard_map/ppermute | solution.py:27
  21.2 4.8 %collective-permute-start.4 = (f32[25,2048]{1,0:T(8,128)S(1)}, f32[25,2048]{1,0:T(8,128)S(1)}, u32[]{:S(2)}, u32[]{:S(2)}) collective-permute-start(f32[25,2048]{1,0:T(8,128)S(1)} %collective-permute-done.3), channel_id=1, source_target_pairs={{0,64},{64,128},{128,192},{192,0},{1,65},{65,129},{129,193},{193,1... | collective-permute-start | bytes 614408 | tf_op jit(solution)/shard_map/ppermute | solution.py:29
  26.0 0.8 collective-permute-done.2
  26.7 7.5 %collective-permute-done.4 = f32[25,2048]{1,0:T(8,128)S(1)} collective-permute-done((f32[25,2048]{1,0:T(8,128)S(1)}, f32[25,2048]{1,0:T(8,128)S(1)}, u32[]{:S(2)}, u32[]{:S(2)}) %collective-permute-start.4) | collective-permute-done | bytes 204832 | tf_op jit(solution)/shard_map/ppermute | solution.py:29
  34.2 2.0 maximum_bitcast_fusion
  36.2 0.0 all-gather.3.cloned.1.call-update
  36.2 0.0 copy-done.2
  36.2 1.7 copy.8
  37.9 2.4 %copy.9 = f32[320,10,100]{2,1,0:T(8,128)S(1)} copy(f32[320,10,100]{2,0,1:T(8,128)} %bitcast.51) | data formatting | bytes 2560000 | tf_op jit(solution)/shard_map/transpose | solution.py:17
  40.4 4.1 %reshape.35 = f32[64,1,5000]{2,1,0:T(1,128)} reshape(f32[320,10,100]{2,1,0:T(8,128)S(1)} %copy.9) | data formatting | bytes 2560000
  44.4 49.0 %all_to_all.15 = f32[64,1,5000]{2,1,0:T(1,128)S(1)} all-to-all(f32[64,1,5000]{2,1,0:T(1,128)} %reshape.35), channel_id=1, replica_groups=mesh['zh'=4,'y'=4,'x'=4,'zl'=2,'core'=2] {'zh','y','x'}, dimensions={0} | all-to-all | bytes 2560000 | tf_op jit(solution)/shard_map/all_to_all | solution.py:18
  93.4 0.6 broadcast.4
  94.0 5.2 %reduce = f32[64,5000]{1,0:T(8,128)} reduce(f32[64,1,5000]{2,1,0:T(1,128)S(1)} %all_to_all.15, f32[]{:T(128)} %broadcast.4), dimensions={1}, to_apply=%all_to_all.11.reduce_sub_computation | reduce | bytes 2560004 | tf_op jit(solution)/shard_map/all_to_all | solution.py:18
  99.2 2.7 %reshape.36 = f32[320,10,100]{2,1,0:T(8,128)S(1)} reshape(f32[64,5000]{1,0:T(8,128)} %reduce) | data formatting | bytes 2560000
  101.9 1.7 copy.11
  103.6 4.8 %reshape.26 = f32[5,10,160,40]{3,2,1,0:T(8,128)} reshape(f32[5,10,64,100]{3,2,1,0:T(8,128)} %copy.11) | data formatting | bytes 2560000 | tf_op jit(solution)/shard_map/reshape | solution.py:20
  108.3 5.2 %copy.12 = f32[5,160,10,40]{1,0,3,2:T(8,128)S(1)} copy(f32[5,160,10,40]{3,1,2,0:T(8,128)} %bitcast.49) | data formatting | bytes 2560000 | tf_op jit(solution)/shard_map/transpose | solution.py:20
  113.5 1.8 reshape.27
  115.3 0.0 collective-permute-start
  115.3 1.8 stack_reshape.3
  117.2 30.7 %collective-permute-done = f32[800,400]{0,1:T(8,128)} collective-permute-done((f32[800,400]{0,1:T(8,128)}, f32[800,400]{0,1:T(8,128)}, u32[]{:S(2)}, u32[]{:S(2)}) %collective-permute-start) | collective-permute-done | bytes 1280032 | tf_op jit(solution)/shard_map/ppermute | solution.py:38
  147.9 0.0 copy-start
  147.9 3.7 %pad_maximum_fusion.1 = f32[2,800,400]{1,2,0:T(8,128)} fusion(f32[1,800,400]{1,2,0:T(8,128)} %bitcast.6, f32[1,800,400]{1,2,0:T(8,128)} %stack_reshape.3), kind=kLoop, calls=%fused_computation.1 | loop fusion | flops 640000 | bytes 5120000 | tf_op jit(solution)/shard_map/stack | solution.py:39
  151.5 1.6 collective-permute-start.1
  153.2 5.2 %collective-permute-done.1 = f32[2,800,400]{1,2,0:T(8,128)} collective-permute-done((f32[2,800,400]{1,2,0:T(8,128)}, f32[2,800,400]{1,2,0:T(8,128)}, u32[]{:S(2)}, u32[]{:S(2)}) %collective-permute-start.1) | collective-permute-done | bytes 2560032 | tf_op jit(solution)/shard_map/ppermute | solution.py:40
  158.4 0.0 copy-done
  158.4 4.5 %select_select_fusion.3 = (f32[800,400]{0,1:T(8,128)}, f32[800,400]{0,1:T(8,128)}, f32[800,400]{0,1:T(8,128)}) fusion(f32[800,400]{0,1:T(8,128)S(1)} %copy-done, f32[800,400]{0,1:T(8,128)} %collective-permute-done, f32[2,800,400]{1,2,0:T(8,128)} %collective-permute-done.1, pred[]{:T(512)S(6)} %eq.38, pred[]{:T(512)S(6)} %eq.37, pred[]{:T(512)S(6)} %eq.36, ...), kind=kLoop, calls=%fused_computation.7 | loop fusion | flops 2880000 | bytes 8960009 | tf_op jit(solution)/shard_map/jit(_where)/select_n | solution.py:46
  162.9 1.5 reshape.28
  164.5 3.1 %select_select_fusion.2 = f32[800,400]{0,1:T(8,128)} fusion(f32[800,400]{0,1:T(8,128)S(1)} %copy-done, f32[800,400]{0,1:T(8,128)} %collective-permute-done, f32[2,800,400]{1,2,0:T(8,128)} %collective-permute-done.1, pred[]{:T(512)S(6)} %eq.41, pred[]{:T(512)S(6)} %eq.40, pred[]{:T(512)S(6)} %eq.39), kind=kLoop, calls=%fused_computation.6 | loop fusion | flops 960000 | bytes 6400003 | tf_op jit(solution)/shard_map/jit(_where)/select_n | solution.py:46
  167.6 2.8 %reshape.29 = f32[800,16,1,25]{0,3,1,2:T(8,128)} reshape(f32[800,400]{0,1:T(8,128)} %select_select_fusion.2) | data formatting | bytes 2560000 | tf_op jit(solution)/shard_map/reshape | solution.py:47
  170.4 0.0 copy-start.1
  170.4 2.9 %reshape.31 = f32[800,16,1,25]{0,3,1,2:T(8,128)} reshape(f32[800,400]{0,1:T(8,128)} %get-tuple-element.6) | data formatting | bytes 2560000 | tf_op jit(solution)/shard_map/reshape | solution.py:47
  173.3 0.0 copy-done.1
  173.3 1.4 reshape.30
  174.7 2.9 %pad_maximum_fusion = f32[800,16,4,25]{0,3,1,2:T(8,128)S(1)} fusion(f32[800,16,1,25]{0,3,1,2:T(8,128)} %reshape.31, f32[800,16,1,25]{0,3,1,2:T(8,128)} %reshape.30, f32[800,16,1,25]{0,3,1,2:T(8,128)} %reshape.29, f32[800,16,1,25]{0,3,1,2:T(8,128)S(1)} %reshape.28), kind=kLoop, calls=%fused_computation | loop fusion | flops 3840000 | bytes 10240000 | tf_op jit(solution)/shard_map/concatenate | solution.py:48
  177.6 3.5 %copy.14 = f32[800,16,4,25]{0,3,2,1:T(8,128)} copy(f32[800,16,4,25]{0,3,1,2:T(8,128)S(1)} %pad_maximum_fusion) | data formatting | bytes 10240000 | tf_op jit(solution)/shard_map/concatenate | solution.py:48
  181.2 6.1 %reshape.32 = f32[800,1600]{0,1:T(8,128)} reshape(f32[800,16,4,25]{0,3,2,1:T(8,128)} %copy.14) | data formatting | bytes 10240000 | tf_op jit(solution)/shard_map/reshape | solution.py:48
  187.2 0.0 all-gather.3.cloned.1.call-done
  187.2 12.0 %reshape.34 = f32[1600,2048]{1,0:T(8,128)} reshape(f32[16,100,2048]{2,1,0:T(8,128)} %all-gather.3.cloned.1.call-done) | data formatting | bytes 26214400
  199.2 25.7 %fusion = f32[800,2048]{1,0:T(8,128)} fusion(f32[800,1600]{0,1:T(8,128)} %reshape.32, f32[1600,2048]{1,0:T(8,128)} %reshape.34), kind=kOutput, calls=%fused_computation.9 | convolution fusion | flops 15728640000 | bytes 24780800 | tf_op jit(solution)/shard_map/dot_general | solution.py:65
Async XLA Ops:
  6.5 29.7 %copy-start.2 = (f32[100,3200]{1,0:T(8,128)S(1)}, f32[100,3200]{1,0:T(8,128)}, u32[]{:S(2)}) copy-start(f32[100,3200]{1,0:T(8,128)} %param.2) | copy-start | bytes 3840004
  6.5 180.7 %all-gather.3.cloned.1.call-start = ((), (), s32[]{:S(2)}) async-start(), calls=%async_computation.1 | async-start | bytes 14483456 | tf_op jit(solution)/shard_map/all_gather | solution.py:63
  6.5 14.6 %collective-permute-start.3 = (f32[25,2048]{1,0:T(8,128)}, f32[25,2048]{1,0:T(8,128)S(1)}, u32[]{:S(2)}, u32[]{:S(2)}) collective-permute-start(f32[25,2048]{1,0:T(8,128)} %param.3), channel_id=1, source_target_pairs={{0,64},{64,128},{128,192},{192,0},{1,65},{65,129},{129,193},{193,1... | collective-permute-start | bytes 614408 | tf_op jit(solution)/shard_map/ppermute | solution.py:27
  10.3 16.4 %collective-permute-start.2 = (f32[25,2048]{1,0:T(8,128)}, f32[25,2048]{1,0:T(8,128)S(1)}, u32[]{:S(2)}, u32[]{:S(2)}) collective-permute-start(f32[25,2048]{1,0:T(8,128)} %param.3), channel_id=1, source_target_pairs={{0,192},{64,0},{128,64},{192,128},{1,193},{65,1},{129,65},{193,129... | collective-permute-start | bytes 614408 | tf_op jit(solution)/shard_map/ppermute | solution.py:28
  21.2 13.1 %collective-permute-start.4 = (f32[25,2048]{1,0:T(8,128)S(1)}, f32[25,2048]{1,0:T(8,128)S(1)}, u32[]{:S(2)}, u32[]{:S(2)}) collective-permute-start(f32[25,2048]{1,0:T(8,128)S(1)} %collective-permute-done.3), channel_id=1, source_target_pairs={{0,64},{64,128},{128,192},{192,0},{1,65},{65,129},{129,193},{193,1... | collective-permute-start | bytes 614408 | tf_op jit(solution)/shard_map/ppermute | solution.py:29
  115.3 32.5 %collective-permute-start = (f32[800,400]{0,1:T(8,128)}, f32[800,400]{0,1:T(8,128)}, u32[]{:S(2)}, u32[]{:S(2)}) collective-permute-start(f32[800,400]{0,1:T(8,128)} %reshape.27), channel_id=1, source_target_pairs={{0,2},{2,0},{1,3},{3,1},{4,6},{6,4},{5,7},{7,5},{8,10},{10,8},{9,1... | collective-permute-start | bytes 3840008 | tf_op jit(solution)/shard_map/ppermute | solution.py:38
  147.9 10.5 %copy-start = (f32[800,400]{0,1:T(8,128)S(1)}, f32[800,400]{0,1:T(8,128)}, u32[]{:S(2)}) copy-start(f32[800,400]{0,1:T(8,128)} %reshape.27) | copy-start | bytes 3840004
  151.5 6.9 %collective-permute-start.1 = (f32[2,800,400]{1,2,0:T(8,128)}, f32[2,800,400]{1,2,0:T(8,128)}, u32[]{:S(2)}, u32[]{:S(2)}) collective-permute-start(f32[2,800,400]{1,2,0:T(8,128)} %pad_maximum_fusion.1), channel_id=1, source_target_pairs={{0,1},{1,0},{2,3},{3,2},{4,5},{5,4},{6,7},{7,6},{8,9},{9,8},{10,11... | collective-permute-start | bytes 7680008 | tf_op jit(solution)/shard_map/ppermute | solution.py:40
  170.4 2.9 %copy-start.1 = (f32[800,400]{0,1:T(8,128)S(1)}, f32[800,400]{0,1:T(8,128)}, u32[]{:S(2)}) copy-start(f32[800,400]{0,1:T(8,128)} %get-tuple-element.7) | copy-start | bytes 3840004
Sparse Core Ops, SparseCore 0:
  36.3 119.4 all-gather.2

commit v2 on v1

--- a/solution.py
+++ b/solution.py
@@ -24,10 +24,11 @@
 def ring_zh(part):
     right = [(i, (i + 1) % 4) for i in range(4)]
     left = [(i, (i - 1) % 4) for i in range(4)]
+    across = [(i, (i + 2) % 4) for i in range(4)]
     from_left = lax.ppermute(part, "zh", right)
     from_right = lax.ppermute(part, "zh", left)
-    from_far = lax.ppermute(from_left, "zh", right)
-    return jnp.concatenate([part, from_right, from_far, from_left], axis=0)
+    from_far = lax.ppermute(part, "zh", across)
+    return jnp.stack([part, from_right, from_far, from_left])
 
 
 def exchange_col(block, slots):
@@ -44,8 +45,8 @@
     for s in range(4):
         d = jnp.bitwise_xor(me, lax.rem(s + zh, 4))
         pick = jnp.where(d == 0, by_d[0], jnp.where(d == 1, by_d[1], jnp.where(d == 2, by_d[2], by_d[3])))
-        outs.append(pick.reshape(rows, slots[0], 1, slots[1]))
-    return jnp.concatenate(outs, axis=2).reshape(rows, 4 * width)
+        outs.append(pick)
+    return jnp.concatenate(outs, axis=1)
 
 
 def local(amplitudes, intermediate):
@@ -59,8 +60,8 @@
     step = cols // CHUNKS
     outs = []
     for c in range(CHUNKS):
-        part = ringed[:, c * step:(c + 1) * step]
-        part = lax.all_gather(part, ("y", "x"), axis=0, tiled=True)
+        part = ringed[:, :, c * step:(c + 1) * step]
+        part = lax.all_gather(part, ("y", "x"), axis=1, tiled=True).reshape(-1, step)
         outs.append(
             jnp.dot(regrouped, part, precision=lax.Precision.HIGH, preferred_element_type=jnp.float32)
         )

time: 232 us -> 214 us (0.922)
  local copies, waits for them, and re-layouts: 57 us -> 45.3 us
  blocking collectives: 49 us -> 42.8 us
  waiting for transfers between devices: 52 us -> 56.5 us
  other arithmetic: 21.4 us -> 17.1 us
    all_gather x0 -> x1, local copies, waits for them, and re-layouts: none -> 17.1 us  [local(): lax.all_gather(part, ('y', 'x'), axis=1, tiled=True).reshape(-1, step)]
    reshape x5 -> x0, local copies, waits for them, and re-layouts: 14.7 us -> none  [the longest x4 8.62 us: exchange_col(): outs.append(pick.reshape(rows, slots[0], 1, slots[1]))]
    unnamed x10 -> x9, local copies, waits for them, and re-layouts: 20.5 us -> 8.37 us
    ppermute x1, waiting for transfers between devices: 0.76 us -> 8.63 us  [ring_zh(): from_right = lax.ppermute(part, 'zh', left)]
    all_to_all x1, blocking collectives: 49 us -> 42.8 us  [regroup_local(): lax.all_to_all(outgoing, ROW, split_axis=0, concat_axis=2, tiled=True)]
    ppermute x1, waiting for transfers between devices: 7.77 us -> 2.18 us  [ring_zh(): from_left = lax.ppermute(part, 'zh', right)]
    concatenate x1 -> x0, local copies, waits for them, and re-layouts: 3.55 us -> none  [exchange_col(): return jnp.concatenate(outs, axis=2).reshape(rows, 4 * width)]
    concatenate x1 -> x0, other arithmetic: 2.9 us -> none  [exchange_col(): return jnp.concatenate(outs, axis=2).reshape(rows, 4 * width)]
  transfers between devices with their start and end apart: 6 -> 6, of which waited for: 5 -> 5; matrix products, arithmetic and copies ran while one was open for 28% -> 20% of each run, Pallas kernels for 0% -> 0%
where the time goes in v2:
time: 214 us; the launch traced here: 213 us
  waiting for transfers between devices  56.5 us (26%)
  local copies, waits for them, and re-layouts  45.3 us (21%)
  blocking collectives  42.8 us (20%)
  matrix products  25.1 us (12%)
  other arithmetic  17.1 us (8%)
  between operations  13.5 us (6%)
  starting transfers between devices  12.9 us (6%)
    all_to_all x1, blocking collectives, regroup_local(): lax.all_to_all(outgoing, ROW, split_axis=0, concat_axis=2, tiled=True)  42.8 us
    ppermute x1, waiting for transfers between devices, exchange_col(): from_zl = lax.ppermute(block, 'zl', [(0, 1), (1, 0)])  30.8 us
    dot_general x1, matrix products, local(): jnp.dot(regrouped, part, precision=lax.Precision.HIGH, preferred_element_...  25.1 us
    all_gather x1, local copies, waits for them, and re-layouts, local(): lax.all_gather(part, ('y', 'x'), axis=1, tiled=True).reshape(-1, step)  17.1 us
    ppermute x1, waiting for transfers between devices, ring_zh(): from_far = lax.ppermute(part, 'zh', across)  9.7 us
    ppermute x1, waiting for transfers between devices, ring_zh(): from_right = lax.ppermute(part, 'zh', left)  8.63 us
    unnamed x9, local copies, waits for them, and re-layouts  8.37 us
    select_n x2, other arithmetic, exchange_col(): jnp.where(d == 0, by_d[0], jnp.where(d == 1, by_d[1], jnp.where(d == 2, b...  6.58 us
  transfers between devices with their start and end apart: 6, of which 5 were waited for; matrix products, arithmetic and copies ran while one was open for 20% of the time, Pallas kernels for 0%

profile of v2, /device:TPU:1, one launch (start us, length us, event | category | flops | bytes accessed | tf_op | source)
XLA Modules:
  0.0 213.2 jit_solution(13934383724822891099)
XLA Ops:
  6.5 0.0 all-gather.2.cloned.1.call-start
  6.5 3.8 %collective-permute-start.4 = (f32[25,2048]{1,0:T(8,128)}, f32[25,2048]{1,0:T(8,128)S(1)}, u32[]{:S(2)}, u32[]{:S(2)}) collective-permute-start(f32[25,2048]{1,0:T(8,128)} %param.3), channel_id=1, source_target_pairs={{0,64},{64,128},{128,192},{192,0},{1,65},{65,129},{129,193},{193,1... | collective-permute-start | bytes 614408 | tf_op jit(solution)/shard_map/ppermute | solution.py:28
  10.3 5.1 %collective-permute-start.3 = (f32[25,2048]{1,0:T(8,128)}, f32[25,2048]{1,0:T(8,128)S(1)}, u32[]{:S(2)}, u32[]{:S(2)}) collective-permute-start(f32[25,2048]{1,0:T(8,128)} %param.3), channel_id=1, source_target_pairs={{0,128},{64,192},{128,0},{192,64},{1,129},{65,193},{129,1},{193,65... | collective-permute-start | bytes 614408 | tf_op jit(solution)/shard_map/ppermute | solution.py:30
  15.5 2.4 %collective-permute-start.2 = (f32[25,2048]{1,0:T(8,128)}, f32[25,2048]{1,0:T(8,128)S(1)}, u32[]{:S(2)}, u32[]{:S(2)}) collective-permute-start(f32[25,2048]{1,0:T(8,128)} %param.3), channel_id=1, source_target_pairs={{0,192},{64,0},{128,64},{192,128},{1,193},{65,1},{129,65},{193,129... | collective-permute-start | bytes 614408 | tf_op jit(solution)/shard_map/ppermute | solution.py:29
  17.8 1.1 stack.23
  19.0 2.2 %collective-permute-done.4 = f32[25,2048]{1,0:T(8,128)S(1)} collective-permute-done((f32[25,2048]{1,0:T(8,128)}, f32[25,2048]{1,0:T(8,128)S(1)}, u32[]{:S(2)}, u32[]{:S(2)}) %collective-permute-start.4) | collective-permute-done | bytes 204832 | tf_op jit(solution)/shard_map/ppermute | solution.py:28
  21.2 0.1 stack.26
  21.3 9.7 %collective-permute-done.3 = f32[25,2048]{1,0:T(8,128)S(1)} collective-permute-done((f32[25,2048]{1,0:T(8,128)}, f32[25,2048]{1,0:T(8,128)S(1)}, u32[]{:S(2)}, u32[]{:S(2)}) %collective-permute-start.3) | collective-permute-done | bytes 204832 | tf_op jit(solution)/shard_map/ppermute | solution.py:30
  31.0 0.1 stack.25
  31.1 0.0 copy-start.2
  31.1 8.6 %collective-permute-done.2 = f32[25,2048]{1,0:T(8,128)S(1)} collective-permute-done((f32[25,2048]{1,0:T(8,128)}, f32[25,2048]{1,0:T(8,128)S(1)}, u32[]{:S(2)}, u32[]{:S(2)}) %collective-permute-start.2) | collective-permute-done | bytes 204832 | tf_op jit(solution)/shard_map/ppermute | solution.py:29
  39.8 0.1 stack.24
  39.9 1.8 pad_maximum_fusion.1
  41.7 0.0 all-gather.2.cloned.1.call-update
  41.7 0.0 copy-done.2
  41.7 1.7 copy.13
  43.4 2.4 %copy.14 = f32[320,10,100]{2,1,0:T(8,128)S(1)} copy(f32[320,10,100]{2,0,1:T(8,128)} %bitcast.40) | data formatting | bytes 2560000 | tf_op jit(solution)/shard_map/transpose | solution.py:17
  45.9 4.1 %reshape.17 = f32[64,1,5000]{2,1,0:T(1,128)} reshape(f32[320,10,100]{2,1,0:T(8,128)S(1)} %copy.14) | data formatting | bytes 2560000
  49.9 42.8 %all_to_all.15 = f32[64,1,5000]{2,1,0:T(1,128)S(1)} all-to-all(f32[64,1,5000]{2,1,0:T(1,128)} %reshape.17), channel_id=1, replica_groups=mesh['zh'=4,'y'=4,'x'=4,'zl'=2,'core'=2] {'zh','y','x'}, dimensions={0} | all-to-all | bytes 2560000 | tf_op jit(solution)/shard_map/all_to_all | solution.py:18
  92.8 0.5 broadcast.4
  93.3 5.1 %reduce = f32[64,5000]{1,0:T(8,128)} reduce(f32[64,1,5000]{2,1,0:T(1,128)S(1)} %all_to_all.15, f32[]{:T(128)} %broadcast.4), dimensions={1}, to_apply=%all_to_all.11.reduce_sub_computation | reduce | bytes 2560004 | tf_op jit(solution)/shard_map/all_to_all | solution.py:18
  98.4 2.6 %reshape.18 = f32[320,10,100]{2,1,0:T(8,128)S(1)} reshape(f32[64,5000]{1,0:T(8,128)} %reduce) | data formatting | bytes 2560000
  101.0 1.7 copy.16
  102.7 4.7 %reshape.14 = f32[5,10,160,40]{3,2,1,0:T(8,128)} reshape(f32[5,10,64,100]{3,2,1,0:T(8,128)} %copy.16) | data formatting | bytes 2560000 | tf_op jit(solution)/shard_map/reshape | solution.py:20
  107.4 5.2 %copy.17 = f32[5,160,10,40]{1,0,3,2:T(8,128)S(1)} copy(f32[5,160,10,40]{3,1,2,0:T(8,128)} %bitcast.37) | data formatting | bytes 2560000 | tf_op jit(solution)/shard_map/transpose | solution.py:20
  112.6 1.8 reshape.15
  114.5 0.0 collective-permute-start
  114.5 1.8 stack_reshape.3
  116.2 30.8 %collective-permute-done = f32[800,400]{0,1:T(8,128)} collective-permute-done((f32[800,400]{0,1:T(8,128)}, f32[800,400]{0,1:T(8,128)}, u32[]{:S(2)}, u32[]{:S(2)}) %collective-permute-start) | collective-permute-done | bytes 1280032 | tf_op jit(solution)/shard_map/ppermute | solution.py:39
  147.0 0.0 copy-start
  147.0 3.7 %pad_maximum_fusion = f32[2,800,400]{1,2,0:T(8,128)} fusion(f32[1,800,400]{1,2,0:T(8,128)} %bitcast.6, f32[1,800,400]{1,2,0:T(8,128)} %stack_reshape.3), kind=kLoop, calls=%fused_computation.8 | loop fusion | flops 640000 | bytes 5120000 | tf_op jit(solution)/shard_map/stack | solution.py:40
  150.7 1.6 collective-permute-start.1
  152.3 5.2 %collective-permute-done.1 = f32[2,800,400]{1,2,0:T(8,128)} collective-permute-done((f32[2,800,400]{1,2,0:T(8,128)}, f32[2,800,400]{1,2,0:T(8,128)}, u32[]{:S(2)}, u32[]{:S(2)}) %collective-permute-start.1) | collective-permute-done | bytes 2560032 | tf_op jit(solution)/shard_map/ppermute | solution.py:41
  157.5 0.0 copy-done
  157.5 2.0 select_select_fusion.2
  159.5 4.5 %select_select_fusion.3 = (f32[800,400]{0,1:T(8,128)}, f32[800,400]{0,1:T(8,128)}, f32[800,400]{0,1:T(8,128)}) fusion(f32[800,400]{0,1:T(8,128)S(1)} %copy-done, f32[800,400]{0,1:T(8,128)} %collective-permute-done, f32[2,800,400]{1,2,0:T(8,128)} %collective-permute-done.1, pred[]{:T(512)S(6)} %eq.38, pred[]{:T(512)S(6)} %eq.37, pred[]{:T(512)S(6)} %eq.36, ...), kind=kLoop, calls=%fused_computation.14 | loop fusion | flops 2880000 | bytes 8960009 | tf_op jit(solution)/shard_map/jit(_where)/select_n | solution.py:47
  164.1 0.0 copy-start.1
  164.1 0.0 all-gather.2.cloned.1.call-done
  164.1 17.1 %copy.19 = f32[4,400,2048]{2,1,0:T(8,128)} copy(f32[4,400,2048]{2,0,1:T(4,128)} %all-gather.2.cloned.1.call-done) | data formatting | bytes 26214400 | tf_op jit(solution)/shard_map/all_gather | solution.py:64
  181.2 0.0 copy-done.1
  181.2 25.1 %fusion = f32[800,2048]{1,0:T(8,128)} fusion(f32[1600,2048]{1,0:T(8,128)} %bitcast.38, f32[800,400]{0,1:T(8,128)} %get-tuple-element.6, f32[800,400]{0,1:T(8,128)} %get-tuple-element.7, f32[800,400]{0,1:T(8,128)S(1)} %select_select_fusion.2, f32[800,400]{0,1:T(8,128)S(1)} %copy-done.1), kind=kOutput, calls=%fused_computation | convolution fusion | flops 15732480000 | bytes 24780800 | tf_op jit(solution)/shard_map/dot_general | solution.py:66
Async XLA Ops:
  6.5 157.6 %all-gather.2.cloned.1.call-start = ((), (), s32[]{:S(2)}) async-start(), calls=%async_computation.1 | async-start | bytes 13926400 | tf_op jit(solution)/shard_map/all_gather | solution.py:64
  6.5 14.6 %collective-permute-start.4 = (f32[25,2048]{1,0:T(8,128)}, f32[25,2048]{1,0:T(8,128)S(1)}, u32[]{:S(2)}, u32[]{:S(2)}) collective-permute-start(f32[25,2048]{1,0:T(8,128)} %param.3), channel_id=1, source_target_pairs={{0,64},{64,128},{128,192},{192,0},{1,65},{65,129},{129,193},{193,1... | collective-permute-start | bytes 614408 | tf_op jit(solution)/shard_map/ppermute | solution.py:28
  10.3 20.6 %collective-permute-start.3 = (f32[25,2048]{1,0:T(8,128)}, f32[25,2048]{1,0:T(8,128)S(1)}, u32[]{:S(2)}, u32[]{:S(2)}) collective-permute-start(f32[25,2048]{1,0:T(8,128)} %param.3), channel_id=1, source_target_pairs={{0,128},{64,192},{128,0},{192,64},{1,129},{65,193},{129,1},{193,65... | collective-permute-start | bytes 614408 | tf_op jit(solution)/shard_map/ppermute | solution.py:30
  15.5 24.3 %collective-permute-start.2 = (f32[25,2048]{1,0:T(8,128)}, f32[25,2048]{1,0:T(8,128)S(1)}, u32[]{:S(2)}, u32[]{:S(2)}) collective-permute-start(f32[25,2048]{1,0:T(8,128)} %param.3), channel_id=1, source_target_pairs={{0,192},{64,0},{128,64},{192,128},{1,193},{65,1},{129,65},{193,129... | collective-permute-start | bytes 614408 | tf_op jit(solution)/shard_map/ppermute | solution.py:29
  31.1 10.6 %copy-start.2 = (f32[100,3200]{1,0:T(8,128)S(1)}, f32[100,3200]{1,0:T(8,128)}, u32[]{:S(2)}) copy-start(f32[100,3200]{1,0:T(8,128)} %param.2) | copy-start | bytes 3840004
  114.5 32.6 %collective-permute-start = (f32[800,400]{0,1:T(8,128)}, f32[800,400]{0,1:T(8,128)}, u32[]{:S(2)}, u32[]{:S(2)}) collective-permute-start(f32[800,400]{0,1:T(8,128)} %reshape.15), channel_id=1, source_target_pairs={{0,2},{2,0},{1,3},{3,1},{4,6},{6,4},{5,7},{7,5},{8,10},{10,8},{9,1... | collective-permute-start | bytes 3840008 | tf_op jit(solution)/shard_map/ppermute | solution.py:39
  147.0 10.5 %copy-start = (f32[800,400]{0,1:T(8,128)S(1)}, f32[800,400]{0,1:T(8,128)}, u32[]{:S(2)}) copy-start(f32[800,400]{0,1:T(8,128)} %reshape.15) | copy-start | bytes 3840004
  150.7 6.8 %collective-permute-start.1 = (f32[2,800,400]{1,2,0:T(8,128)}, f32[2,800,400]{1,2,0:T(8,128)}, u32[]{:S(2)}, u32[]{:S(2)}) collective-permute-start(f32[2,800,400]{1,2,0:T(8,128)} %pad_maximum_fusion), channel_id=1, source_target_pairs={{0,1},{1,0},{2,3},{3,2},{4,5},{5,4},{6,7},{7,6},{8,9},{9,8},{10,11... | collective-permute-start | bytes 7680008 | tf_op jit(solution)/shard_map/ppermute | solution.py:41
  164.1 17.2 %copy-start.1 = (f32[800,400]{0,1:T(8,128)S(1)}, f32[800,400]{0,1:T(8,128)}, u32[]{:S(2)}) copy-start(f32[800,400]{0,1:T(8,128)} %get-tuple-element.5) | copy-start | bytes 3840004
Sparse Core Ops, SparseCore 0:
  41.8 110.2 all-gather.1

commit v3 on v2

--- a/solution.py
+++ b/solution.py
@@ -36,10 +36,11 @@
     core = lax.axis_index("core")
     zh = lax.axis_index("zh")
     me = zl * 2 + core
-    from_zl = lax.ppermute(block, "zl", [(0, 1), (1, 0)])
-    pair = jnp.stack([block, from_zl])
-    from_core = lax.ppermute(pair, "core", [(0, 1), (1, 0)])
-    by_d = (block, from_core[0], from_zl, from_core[1])
+    swap = [(0, 1), (1, 0)]
+    from_zl = lax.ppermute(block, "zl", swap)
+    from_core = lax.ppermute(block, "core", swap)
+    from_both = lax.ppermute(from_zl, "core", swap)
+    by_d = (block, from_core, from_zl, from_both)
     rows, width = block.shape
     outs = []
     for s in range(4):

time: 214 us -> 206 us (0.963)
  other arithmetic: 17.1 us -> 11.7 us
    another operation x1 -> x0, other arithmetic: 3.66 us -> none  [exchange_col(): pair = jnp.stack([block, from_zl])]
    select_n x2 -> x1, other arithmetic: 6.58 us -> 4.77 us  [exchange_col(): jnp.where(d == 0, by_d[0], jnp.where(d == 1, by_d[1], jnp.where(d == 2, b...]
    ppermute x2 -> x3, waiting for transfers between devices: 36 us -> 34.8 us  [the longest x1 31.8 us: exchange_col(): from_zl = lax.ppermute(block, 'zl', swap)]
  transfers between devices with their start and end apart: 6 -> 7, of which waited for: 5 -> 5; matrix products, arithmetic and copies ran while one was open for 20% -> 18% of each run, Pallas kernels for 0% -> 0%
where the time goes in v3:
time: 206 us; the launch traced here: 205 us
  waiting for transfers between devices  55.3 us (27%)
  local copies, waits for them, and re-layouts  43.5 us (21%)
  blocking collectives  42.8 us (21%)
  matrix products  25.2 us (12%)
  starting transfers between devices  13.5 us (7%)
  between operations  13.5 us (7%)
  other arithmetic  11.7 us (6%)
    all_to_all x1, blocking collectives, regroup_local(): lax.all_to_all(outgoing, ROW, split_axis=0, concat_axis=2, tiled=True)  42.8 us
    ppermute x1, waiting for transfers between devices, exchange_col(): from_zl = lax.ppermute(block, 'zl', swap)  31.8 us
    dot_general x1, matrix products, local(): jnp.dot(regrouped, part, precision=lax.Precision.HIGH, preferred_element_...  25.2 us
    all_gather x1, local copies, waits for them, and re-layouts, local(): lax.all_gather(part, ('y', 'x'), axis=1, tiled=True).reshape(-1, step)  17.2 us
    ppermute x1, waiting for transfers between devices, ring_zh(): from_far = lax.ppermute(part, 'zh', across)  9.7 us
    ppermute x1, waiting for transfers between devices, ring_zh(): from_right = lax.ppermute(part, 'zh', left)  8.63 us
    unnamed x9, local copies, waits for them, and re-layouts  8.37 us
    transpose x1, local copies, waits for them, and re-layouts, regroup_local(): received.reshape(virt_local, b_count, set_rows, O).transpose(0, 2, 1, 3)  5.2 us
  transfers between devices with their start and end apart: 7, of which 5 were waited for; matrix products, arithmetic and copies ran while one was open for 18% of the time, Pallas kernels for 0%

profile of v3, /device:TPU:1, one launch (start us, length us, event | category | flops | bytes accessed | tf_op | source)
XLA Modules:
  0.0 205.5 jit_solution(2778692560101759249)
XLA Ops:
  6.5 0.0 all-gather.2.cloned.1.call-start
  6.5 3.8 %collective-permute-start.5 = (f32[25,2048]{1,0:T(8,128)}, f32[25,2048]{1,0:T(8,128)S(1)}, u32[]{:S(2)}, u32[]{:S(2)}) collective-permute-start(f32[25,2048]{1,0:T(8,128)} %param.3), channel_id=1, source_target_pairs={{0,64},{64,128},{128,192},{192,0},{1,65},{65,129},{129,193},{193,1... | collective-permute-start | bytes 614408 | tf_op jit(solution)/shard_map/ppermute | solution.py:28
  10.3 5.1 %collective-permute-start.4 = (f32[25,2048]{1,0:T(8,128)}, f32[25,2048]{1,0:T(8,128)S(1)}, u32[]{:S(2)}, u32[]{:S(2)}) collective-permute-start(f32[25,2048]{1,0:T(8,128)} %param.3), channel_id=1, source_target_pairs={{0,128},{64,192},{128,0},{192,64},{1,129},{65,193},{129,1},{193,65... | collective-permute-start | bytes 614408 | tf_op jit(solution)/shard_map/ppermute | solution.py:30
  15.5 2.4 %collective-permute-start.3 = (f32[25,2048]{1,0:T(8,128)}, f32[25,2048]{1,0:T(8,128)S(1)}, u32[]{:S(2)}, u32[]{:S(2)}) collective-permute-start(f32[25,2048]{1,0:T(8,128)} %param.3), channel_id=1, source_target_pairs={{0,192},{64,0},{128,64},{192,128},{1,193},{65,1},{129,65},{193,129... | collective-permute-start | bytes 614408 | tf_op jit(solution)/shard_map/ppermute | solution.py:29
  17.8 1.1 stack.15
  19.0 2.2 %collective-permute-done.5 = f32[25,2048]{1,0:T(8,128)S(1)} collective-permute-done((f32[25,2048]{1,0:T(8,128)}, f32[25,2048]{1,0:T(8,128)S(1)}, u32[]{:S(2)}, u32[]{:S(2)}) %collective-permute-start.5) | collective-permute-done | bytes 204832 | tf_op jit(solution)/shard_map/ppermute | solution.py:28
  21.2 0.1 stack.18
  21.3 9.7 %collective-permute-done.4 = f32[25,2048]{1,0:T(8,128)S(1)} collective-permute-done((f32[25,2048]{1,0:T(8,128)}, f32[25,2048]{1,0:T(8,128)S(1)}, u32[]{:S(2)}, u32[]{:S(2)}) %collective-permute-start.4) | collective-permute-done | bytes 204832 | tf_op jit(solution)/shard_map/ppermute | solution.py:30
  31.0 0.1 stack.17
  31.1 0.0 copy-start.2
  31.1 8.6 %collective-permute-done.3 = f32[25,2048]{1,0:T(8,128)S(1)} collective-permute-done((f32[25,2048]{1,0:T(8,128)}, f32[25,2048]{1,0:T(8,128)S(1)}, u32[]{:S(2)}, u32[]{:S(2)}) %collective-permute-start.3) | collective-permute-done | bytes 204832 | tf_op jit(solution)/shard_map/ppermute | solution.py:29
  39.8 0.1 stack.16
  39.9 1.8 pad_maximum_fusion
  41.7 0.0 all-gather.2.cloned.1.call-update
  41.8 0.0 copy-done.2
  41.8 1.7 copy.11
  43.5 2.4 %copy.12 = f32[320,10,100]{2,1,0:T(8,128)S(1)} copy(f32[320,10,100]{2,0,1:T(8,128)} %bitcast.17) | data formatting | bytes 2560000 | tf_op jit(solution)/shard_map/transpose | solution.py:17
  45.9 4.1 %reshape.17 = f32[64,1,5000]{2,1,0:T(1,128)} reshape(f32[320,10,100]{2,1,0:T(8,128)S(1)} %copy.12) | data formatting | bytes 2560000
  50.0 42.8 %all_to_all.15 = f32[64,1,5000]{2,1,0:T(1,128)S(1)} all-to-all(f32[64,1,5000]{2,1,0:T(1,128)} %reshape.17), channel_id=1, replica_groups=mesh['zh'=4,'y'=4,'x'=4,'zl'=2,'core'=2] {'zh','y','x'}, dimensions={0} | all-to-all | bytes 2560000 | tf_op jit(solution)/shard_map/all_to_all | solution.py:18
  92.8 0.5 broadcast.4
  93.3 5.1 %reduce = f32[64,5000]{1,0:T(8,128)} reduce(f32[64,1,5000]{2,1,0:T(1,128)S(1)} %all_to_all.15, f32[]{:T(128)} %broadcast.4), dimensions={1}, to_apply=%all_to_all.11.reduce_sub_computation | reduce | bytes 2560004 | tf_op jit(solution)/shard_map/all_to_all | solution.py:18
  98.4 2.6 %reshape.18 = f32[320,10,100]{2,1,0:T(8,128)S(1)} reshape(f32[64,5000]{1,0:T(8,128)} %reduce) | data formatting | bytes 2560000
  101.0 1.7 copy.14
  102.7 4.7 %reshape.14 = f32[5,10,160,40]{3,2,1,0:T(8,128)} reshape(f32[5,10,64,100]{3,2,1,0:T(8,128)} %copy.14) | data formatting | bytes 2560000 | tf_op jit(solution)/shard_map/reshape | solution.py:20
  107.4 5.2 %copy.15 = f32[5,160,10,40]{1,0,3,2:T(8,128)S(1)} copy(f32[5,160,10,40]{3,1,2,0:T(8,128)} %bitcast.14) | data formatting | bytes 2560000 | tf_op jit(solution)/shard_map/transpose | solution.py:20
  112.7 1.8 reshape.15
  114.5 0.0 collective-permute-start.1
  114.5 0.7 collective-permute-start
  115.2 31.8 %collective-permute-done.1 = f32[800,400]{0,1:T(8,128)S(1)} collective-permute-done((f32[800,400]{0,1:T(8,128)}, f32[800,400]{0,1:T(8,128)S(1)}, u32[]{:S(2)}, u32[]{:S(2)}) %collective-permute-start.1) | collective-permute-done | bytes 1280032 | tf_op jit(solution)/shard_map/ppermute | solution.py:40
  147.0 1.5 collective-permute-start.2
  148.5 0.0 collective-permute-done
  148.5 3.0 %collective-permute-done.2 = f32[800,400]{0,1:T(8,128)} collective-permute-done((f32[800,400]{0,1:T(8,128)S(1)}, f32[800,400]{0,1:T(8,128)}, u32[]{:S(2)}, u32[]{:S(2)}) %collective-permute-start.2) | collective-permute-done | bytes 1280032 | tf_op jit(solution)/shard_map/ppermute | solution.py:42
  151.5 4.8 %select_select_fusion.3 = (f32[800,400]{0,1:T(8,128)}, f32[800,400]{0,1:T(8,128)}, f32[800,400]{0,1:T(8,128)}, f32[800,400]{0,1:T(8,128)}) fusion(f32[800,400]{0,1:T(8,128)} %reshape.15, f32[800,400]{0,1:T(8,128)S(1)} %collective-permute-done, f32[800,400]{0,1:T(8,128)S(1)} %collective-permute-done.1, f32[800,400]{0,1:T(8,128)} %collective-permute-done.2, ...), kind=kLoop, calls=%fused_computation.11 | loop fusion | flops 3840000 | bytes 10240012 | tf_op jit(solution)/shard_map/jit(_where)/select_n | solution.py:48
  156.2 0.0 copy-start
  156.2 0.0 copy-start.1
  156.2 0.0 all-gather.2.cloned.1.call-done
  156.2 17.2 %copy.16 = f32[4,400,2048]{2,1,0:T(8,128)} copy(f32[4,400,2048]{2,0,1:T(4,128)} %all-gather.2.cloned.1.call-done) | data formatting | bytes 26214400 | tf_op jit(solution)/shard_map/all_gather | solution.py:65
  173.4 0.0 copy-done
  173.4 0.0 copy-done.1
  173.5 25.2 %fusion = f32[800,2048]{1,0:T(8,128)} fusion(f32[1600,2048]{1,0:T(8,128)} %bitcast.15, f32[800,400]{0,1:T(8,128)S(1)} %copy-done.1, f32[800,400]{0,1:T(8,128)} %get-tuple-element.7, f32[800,400]{0,1:T(8,128)} %get-tuple-element.8, f32[800,400]{0,1:T(8,128)S(1)} %copy-done), kind=kOutput, calls=%fused_computation | convolution fusion | flops 15732480000 | bytes 24780800 | tf_op jit(solution)/shard_map/dot_general | solution.py:67
Async XLA Ops:
  6.5 149.7 %all-gather.2.cloned.1.call-start = ((), (), s32[]{:S(2)}) async-start(), calls=%async_computation.1 | async-start | bytes 13926400 | tf_op jit(solution)/shard_map/all_gather | solution.py:65
  6.5 14.6 %collective-permute-start.5 = (f32[25,2048]{1,0:T(8,128)}, f32[25,2048]{1,0:T(8,128)S(1)}, u32[]{:S(2)}, u32[]{:S(2)}) collective-permute-start(f32[25,2048]{1,0:T(8,128)} %param.3), channel_id=1, source_target_pairs={{0,64},{64,128},{128,192},{192,0},{1,65},{65,129},{129,193},{193,1... | collective-permute-start | bytes 614408 | tf_op jit(solution)/shard_map/ppermute | solution.py:28
  10.3 20.6 %collective-permute-start.4 = (f32[25,2048]{1,0:T(8,128)}, f32[25,2048]{1,0:T(8,128)S(1)}, u32[]{:S(2)}, u32[]{:S(2)}) collective-permute-start(f32[25,2048]{1,0:T(8,128)} %param.3), channel_id=1, source_target_pairs={{0,128},{64,192},{128,0},{192,64},{1,129},{65,193},{129,1},{193,65... | collective-permute-start | bytes 614408 | tf_op jit(solution)/shard_map/ppermute | solution.py:30
  15.5 24.3 %collective-permute-start.3 = (f32[25,2048]{1,0:T(8,128)}, f32[25,2048]{1,0:T(8,128)S(1)}, u32[]{:S(2)}, u32[]{:S(2)}) collective-permute-start(f32[25,2048]{1,0:T(8,128)} %param.3), channel_id=1, source_target_pairs={{0,192},{64,0},{128,64},{192,128},{1,193},{65,1},{129,65},{193,129... | collective-permute-start | bytes 614408 | tf_op jit(solution)/shard_map/ppermute | solution.py:29
  31.1 10.6 %copy-start.2 = (f32[100,3200]{1,0:T(8,128)S(1)}, f32[100,3200]{1,0:T(8,128)}, u32[]{:S(2)}) copy-start(f32[100,3200]{1,0:T(8,128)} %param.2) | copy-start | bytes 3840004
  114.5 32.6 %collective-permute-start.1 = (f32[800,400]{0,1:T(8,128)}, f32[800,400]{0,1:T(8,128)S(1)}, u32[]{:S(2)}, u32[]{:S(2)}) collective-permute-start(f32[800,400]{0,1:T(8,128)} %reshape.15), channel_id=1, source_target_pairs={{0,2},{2,0},{1,3},{3,1},{4,6},{6,4},{5,7},{7,5},{8,10},{10,8},{9,1... | collective-permute-start | bytes 3840008 | tf_op jit(solution)/shard_map/ppermute | solution.py:40
  114.5 34.0 %collective-permute-start = (f32[800,400]{0,1:T(8,128)}, f32[800,400]{0,1:T(8,128)S(1)}, u32[]{:S(2)}, u32[]{:S(2)}) collective-permute-start(f32[800,400]{0,1:T(8,128)} %reshape.15), channel_id=1, source_target_pairs={{0,1},{1,0},{2,3},{3,2},{4,5},{5,4},{6,7},{7,6},{8,9},{9,8},{10,11... | collective-permute-start | bytes 3840008 | tf_op jit(solution)/shard_map/ppermute | solution.py:41
  147.0 4.4 %collective-permute-start.2 = (f32[800,400]{0,1:T(8,128)S(1)}, f32[800,400]{0,1:T(8,128)}, u32[]{:S(2)}, u32[]{:S(2)}) collective-permute-start(f32[800,400]{0,1:T(8,128)S(1)} %collective-permute-done.1), channel_id=1, source_target_pairs={{0,1},{1,0},{2,3},{3,2},{4,5},{5,4},{6,7},{7,6},{8,9},{9,8},{10,11... | collective-permute-start | bytes 3840008 | tf_op jit(solution)/shard_map/ppermute | solution.py:42
  156.2 17.2 %copy-start = (f32[800,400]{0,1:T(8,128)S(1)}, f32[800,400]{0,1:T(8,128)}, u32[]{:S(2)}) copy-start(f32[800,400]{0,1:T(8,128)} %get-tuple-element.5) | copy-start | bytes 3840004
  156.2 17.2 %copy-start.1 = (f32[800,400]{0,1:T(8,128)S(1)}, f32[800,400]{0,1:T(8,128)}, u32[]{:S(2)}) copy-start(f32[800,400]{0,1:T(8,128)} %get-tuple-element.6) | copy-start | bytes 3840004
Sparse Core Ops, SparseCore 0:
  41.9 110.2 all-gather.1

commit v4 on v3

--- a/solution.py
+++ b/solution.py
@@ -47,7 +47,7 @@
         d = jnp.bitwise_xor(me, lax.rem(s + zh, 4))
         pick = jnp.where(d == 0, by_d[0], jnp.where(d == 1, by_d[1], jnp.where(d == 2, by_d[2], by_d[3])))
         outs.append(pick)
-    return jnp.concatenate(outs, axis=1)
+    return jnp.stack(outs, axis=1)
 
 
 def local(amplitudes, intermediate):
@@ -62,9 +62,12 @@
     outs = []
     for c in range(CHUNKS):
         part = ringed[:, :, c * step:(c + 1) * step]
-        part = lax.all_gather(part, ("y", "x"), axis=1, tiled=True).reshape(-1, step)
+        part = lax.all_gather(part, ("y", "x"), axis=1, tiled=True)
         outs.append(
-            jnp.dot(regrouped, part, precision=lax.Precision.HIGH, preferred_element_type=jnp.float32)
+            lax.dot_general(
+                regrouped, part, (((1, 2), (0, 1)), ((), ())),
+                precision=lax.Precision.HIGH, preferred_element_type=jnp.float32,
+            )
         )
     return jnp.concatenate(outs, axis=1)
 

time: 206 us -> 192 us (0.932)
  local copies, waits for them, and re-layouts: 43.5 us -> 26.4 us
  waiting for transfers between devices: 55.3 us -> 44.1 us
  blocking collectives: 42.8 us -> 49.9 us
  starting transfers between devices: 13.5 us -> 17.2 us
  matrix products: 25.2 us -> 28.6 us
    all_gather x1 -> x0, local copies, waits for them, and re-layouts: 17.2 us -> none  [local(): lax.all_gather(part, ('y', 'x'), axis=1, tiled=True).reshape(-1, step)]
    all_to_all x1, blocking collectives: 42.8 us -> 49.9 us  [regroup_local(): lax.all_to_all(outgoing, ROW, split_axis=0, concat_axis=2, tiled=True)]
    ppermute x1, waiting for transfers between devices: 31.8 us -> 26.9 us  [exchange_col(): from_zl = lax.ppermute(block, 'zl', swap)]
    select_n x1 -> x0, other arithmetic: 4.77 us -> none  [exchange_col(): jnp.where(d == 0, by_d[0], jnp.where(d == 1, by_d[1], jnp.where(d == 2, b...]
    another operation x0 -> x1, other arithmetic: none -> 4.64 us  [exchange_col(): return jnp.stack(outs, axis=1)]
    ppermute x1, starting transfers between devices: 2.38 us -> 6.84 us  [ring_zh(): from_right = lax.ppermute(part, 'zh', left)]
    ppermute x1, starting transfers between devices: 3.81 us -> 0.01 us  [ring_zh(): from_left = lax.ppermute(part, 'zh', right)]
    dot_general x1, matrix products: 25.2 us -> 28.6 us  [local(): lax.dot_general(regrouped, part, (((1, 2), (0, 1)), ((), ())), precision=...]
  transfers between devices with their start and end apart: 7 -> 7, of which waited for: 5 -> 4; matrix products, arithmetic and copies ran while one was open for 18% -> 19% of each run, Pallas kernels for 0% -> 0%
where the time goes in v4:
time: 192 us; the launch traced here: 191 us
  blocking collectives  49.9 us (26%)
  waiting for transfers between devices  44.1 us (23%)
  matrix products  28.6 us (15%)
  local copies, waits for them, and re-layouts  26.4 us (14%)
  starting transfers between devices  17.2 us (9%)
  between operations  13.5 us (7%)
  other arithmetic  11.6 us (6%)
    all_to_all x1, blocking collectives, regroup_local(): lax.all_to_all(outgoing, ROW, split_axis=0, concat_axis=2, tiled=True)  49.9 us
    dot_general x1, matrix products, local(): lax.dot_general(regrouped, part, (((1, 2), (0, 1)), ((), ())), precision=...  28.6 us
    ppermute x1, waiting for transfers between devices, exchange_col(): from_zl = lax.ppermute(block, 'zl', swap)  26.9 us
    unnamed x5, local copies, waits for them, and re-layouts  8.36 us
    ppermute x1, waiting for transfers between devices, ring_zh(): from_right = lax.ppermute(part, 'zh', left)  7.47 us
    ppermute x1, starting transfers between devices, ring_zh(): from_right = lax.ppermute(part, 'zh', left)  6.84 us
    ppermute x1, waiting for transfers between devices, ring_zh(): from_far = lax.ppermute(part, 'zh', across)  6.69 us
    transpose x1, local copies, waits for them, and re-layouts, regroup_local(): received.reshape(virt_local, b_count, set_rows, O).transpose(0, 2, 1, 3)  5.28 us
  transfers between devices with their start and end apart: 7, of which 4 were waited for; matrix products, arithmetic and copies ran while one was open for 19% of the time, Pallas kernels for 0%

profile of v4, /device:TPU:1, one launch (start us, length us, event | category | flops | bytes accessed | tf_op | source)
XLA Modules:
  0.0 191.2 jit_solution(4813767896490724210)
XLA Ops:
  6.5 0.0 all-gather.2.cloned.1.call-start
  6.5 6.8 %collective-permute-start.3 = (f32[25,2048]{1,0:T(8,128)}, f32[25,2048]{1,0:T(8,128)S(1)}, u32[]{:S(2)}, u32[]{:S(2)}) collective-permute-start(f32[25,2048]{1,0:T(8,128)} %param.3), channel_id=1, source_target_pairs={{0,192},{64,0},{128,64},{192,128},{1,193},{65,1},{129,65},{193,129... | collective-permute-start | bytes 614408 | tf_op jit(solution)/shard_map/ppermute | solution.py:29
  13.4 0.0 collective-permute-start.5
  13.4 3.3 %collective-permute-start.4 = (f32[25,2048]{1,0:T(8,128)}, f32[25,2048]{1,0:T(8,128)S(1)}, u32[]{:S(2)}, u32[]{:S(2)}) collective-permute-start(f32[25,2048]{1,0:T(8,128)} %param.3), channel_id=1, source_target_pairs={{0,128},{64,192},{128,0},{192,64},{1,129},{65,193},{129,1},{193,65... | collective-permute-start | bytes 614408 | tf_op jit(solution)/shard_map/ppermute | solution.py:30
  16.6 1.1 stack.35
  17.8 7.5 %collective-permute-done.3 = f32[25,2048]{1,0:T(8,128)S(1)} collective-permute-done((f32[25,2048]{1,0:T(8,128)}, f32[25,2048]{1,0:T(8,128)S(1)}, u32[]{:S(2)}, u32[]{:S(2)}) %collective-permute-start.3) | collective-permute-done | bytes 204832 | tf_op jit(solution)/shard_map/ppermute | solution.py:29
  25.2 0.1 stack.36
  25.4 0.0 collective-permute-done.5
  25.4 0.1 stack.38
  25.5 0.0 copy-start
  25.5 6.7 %collective-permute-done.4 = f32[25,2048]{1,0:T(8,128)S(1)} collective-permute-done((f32[25,2048]{1,0:T(8,128)}, f32[25,2048]{1,0:T(8,128)S(1)}, u32[]{:S(2)}, u32[]{:S(2)}) %collective-permute-start.4) | collective-permute-done | bytes 204832 | tf_op jit(solution)/shard_map/ppermute | solution.py:30
  32.2 0.1 stack.37
  32.4 1.8 pad_maximum_fusion
  34.2 0.0 all-gather.2.cloned.1.call-update
  34.2 0.0 copy-done
  34.2 1.7 copy.6
  35.9 2.4 %copy.7 = f32[320,10,100]{2,1,0:T(8,128)S(1)} copy(f32[320,10,100]{2,0,1:T(8,128)} %bitcast.24) | data formatting | bytes 2560000 | tf_op jit(solution)/shard_map/transpose | solution.py:17
  38.4 4.1 %reshape.14 = f32[64,1,5000]{2,1,0:T(1,128)} reshape(f32[320,10,100]{2,1,0:T(8,128)S(1)} %copy.7) | data formatting | bytes 2560000
  42.4 49.9 %all_to_all.15 = f32[64,1,5000]{2,1,0:T(1,128)S(1)} all-to-all(f32[64,1,5000]{2,1,0:T(1,128)} %reshape.14), channel_id=1, replica_groups=mesh['zh'=4,'y'=4,'x'=4,'zl'=2,'core'=2] {'zh','y','x'}, dimensions={0} | all-to-all | bytes 2560000 | tf_op jit(solution)/shard_map/all_to_all | solution.py:18
  92.4 0.5 broadcast.4
  92.9 5.1 %reduce = f32[64,5000]{1,0:T(8,128)} reduce(f32[64,1,5000]{2,1,0:T(1,128)S(1)} %all_to_all.15, f32[]{:T(128)} %broadcast.4), dimensions={1}, to_apply=%all_to_all.11.reduce_sub_computation | reduce | bytes 2560004 | tf_op jit(solution)/shard_map/all_to_all | solution.py:18
  98.0 2.6 %reshape.15 = f32[320,10,100]{2,1,0:T(8,128)S(1)} reshape(f32[64,5000]{1,0:T(8,128)} %reduce) | data formatting | bytes 2560000
  100.6 1.7 copy.9
  102.3 4.7 %reshape.11 = f32[5,10,160,40]{3,2,1,0:T(8,128)} reshape(f32[5,10,64,100]{3,2,1,0:T(8,128)} %copy.9) | data formatting | bytes 2560000 | tf_op jit(solution)/shard_map/reshape | solution.py:20
  107.0 5.3 %copy.10 = f32[5,160,10,40]{1,0,3,2:T(8,128)S(1)} copy(f32[5,160,10,40]{3,1,2,0:T(8,128)} %bitcast.22) | data formatting | bytes 2560000 | tf_op jit(solution)/shard_map/transpose | solution.py:20
  112.3 1.8 reshape.12
  114.1 0.0 collective-permute-start.1
  114.1 3.2 %collective-permute-start = (f32[800,400]{0,1:T(8,128)}, f32[800,400]{0,1:T(8,128)S(1)}, u32[]{:S(2)}, u32[]{:S(2)}) collective-permute-start(f32[800,400]{0,1:T(8,128)} %reshape.12), channel_id=1, source_target_pairs={{0,1},{1,0},{2,3},{3,2},{4,5},{5,4},{6,7},{7,6},{8,9},{9,8},{10,11... | collective-permute-start | bytes 3840008 | tf_op jit(solution)/shard_map/ppermute | solution.py:41
  117.3 26.9 %collective-permute-done.1 = f32[800,400]{0,1:T(8,128)S(1)} collective-permute-done((f32[800,400]{0,1:T(8,128)}, f32[800,400]{0,1:T(8,128)S(1)}, u32[]{:S(2)}, u32[]{:S(2)}) %collective-permute-start.1) | collective-permute-done | bytes 1280032 | tf_op jit(solution)/shard_map/ppermute | solution.py:40
  144.2 3.9 %collective-permute-start.2 = (f32[800,400]{0,1:T(8,128)S(1)}, f32[800,400]{0,1:T(8,128)}, u32[]{:S(2)}, u32[]{:S(2)}) collective-permute-start(f32[800,400]{0,1:T(8,128)S(1)} %collective-permute-done.1), channel_id=1, source_target_pairs={{0,1},{1,0},{2,3},{3,2},{4,5},{5,4},{6,7},{7,6},{8,9},{9,8},{10,11... | collective-permute-start | bytes 3840008 | tf_op jit(solution)/shard_map/ppermute | solution.py:42
  148.2 0.0 collective-permute-done
  148.2 3.0 %collective-permute-done.2 = f32[800,400]{0,1:T(8,128)} collective-permute-done((f32[800,400]{0,1:T(8,128)S(1)}, f32[800,400]{0,1:T(8,128)}, u32[]{:S(2)}, u32[]{:S(2)}) %collective-permute-start.2) | collective-permute-done | bytes 1280032 | tf_op jit(solution)/shard_map/ppermute | solution.py:42
  151.1 4.6 %select_bitcast_fusion.3 = (f32[800,1,400]{0,2,1:T(8,128)}, f32[800,1,400]{0,2,1:T(8,128)}, f32[800,1,400]{0,2,1:T(8,128)}, f32[800,1,400]{0,2,1:T(8,128)}) fusion(f32[800,400]{0,1:T(8,128)} %reshape.12, f32[800,400]{0,1:T(8,128)S(1)} %collective-permute-done, f32[800,400]{0,1:T(8,128)S(1)} %collective-permute-done.1, f32[800,400]{0,1:T(8,128)} %collective-permute-done.2, ...), kind=kLoop, calls=%fused_computation.13 | loop fusion | flops 3840000 | bytes 10240012 | tf_op jit(solution)/shard_map/stack | solution.py:50
  155.8 0.0 all-gather.2.cloned.1.call-done
  155.8 28.6 %fusion.9 = f32[800,2048]{1,0:T(8,128)} fusion(f32[4,400,2048]{2,0,1:T(4,128)} %all-gather.2.cloned.1.call-done, f32[800,1,400]{0,2,1:T(8,128)} %get-tuple-element.6, f32[800,1,400]{0,2,1:T(8,128)} %get-tuple-element.7, f32[800,1,400]{0,2,1:T(8,128)} %get-tuple-element.8, f32[800,1,400]{0,2,1:T(8,128)} %get-tuple-element.5), kind=kOutput, calls=%fused_computation.9 | convolution fusion | flops 15732480000 | bytes 24780800 | tf_op jit(solution)/shard_map/dot_general | solution.py:67
Async XLA Ops:
  6.5 149.2 %all-gather.2.cloned.1.call-start = ((), (), s32[]{:S(2)}) async-start(), calls=%async_computation.1 | async-start | bytes 13926400 | tf_op jit(solution)/shard_map/all_gather | solution.py:65
  6.5 18.7 %collective-permute-start.3 = (f32[25,2048]{1,0:T(8,128)}, f32[25,2048]{1,0:T(8,128)S(1)}, u32[]{:S(2)}, u32[]{:S(2)}) collective-permute-start(f32[25,2048]{1,0:T(8,128)} %param.3), channel_id=1, source_target_pairs={{0,192},{64,0},{128,64},{192,128},{1,193},{65,1},{129,65},{193,129... | collective-permute-start | bytes 614408 | tf_op jit(solution)/shard_map/ppermute | solution.py:29
  13.4 12.0 %collective-permute-start.5 = (f32[25,2048]{1,0:T(8,128)}, f32[25,2048]{1,0:T(8,128)S(1)}, u32[]{:S(2)}, u32[]{:S(2)}) collective-permute-start(f32[25,2048]{1,0:T(8,128)} %param.3), channel_id=1, source_target_pairs={{0,64},{64,128},{128,192},{192,0},{1,65},{65,129},{129,193},{193,1... | collective-permute-start | bytes 614408 | tf_op jit(solution)/shard_map/ppermute | solution.py:28
  13.4 18.9 %collective-permute-start.4 = (f32[25,2048]{1,0:T(8,128)}, f32[25,2048]{1,0:T(8,128)S(1)}, u32[]{:S(2)}, u32[]{:S(2)}) collective-permute-start(f32[25,2048]{1,0:T(8,128)} %param.3), channel_id=1, source_target_pairs={{0,128},{64,192},{128,0},{192,64},{1,129},{65,193},{129,1},{193,65... | collective-permute-start | bytes 614408 | tf_op jit(solution)/shard_map/ppermute | solution.py:30
  25.5 8.7 %copy-start = (f32[100,3200]{1,0:T(8,128)S(1)}, f32[100,3200]{1,0:T(8,128)}, u32[]{:S(2)}) copy-start(f32[100,3200]{1,0:T(8,128)} %param.2) | copy-start | bytes 3840004
  114.1 30.1 %collective-permute-start.1 = (f32[800,400]{0,1:T(8,128)}, f32[800,400]{0,1:T(8,128)S(1)}, u32[]{:S(2)}, u32[]{:S(2)}) collective-permute-start(f32[800,400]{0,1:T(8,128)} %reshape.12), channel_id=1, source_target_pairs={{0,2},{2,0},{1,3},{3,1},{4,6},{6,4},{5,7},{7,5},{8,10},{10,8},{9,1... | collective-permute-start | bytes 3840008 | tf_op jit(solution)/shard_map/ppermute | solution.py:40
  114.1 34.0 %collective-permute-start = (f32[800,400]{0,1:T(8,128)}, f32[800,400]{0,1:T(8,128)S(1)}, u32[]{:S(2)}, u32[]{:S(2)}) collective-permute-start(f32[800,400]{0,1:T(8,128)} %reshape.12), channel_id=1, source_target_pairs={{0,1},{1,0},{2,3},{3,2},{4,5},{5,4},{6,7},{7,6},{8,9},{9,8},{10,11... | collective-permute-start | bytes 3840008 | tf_op jit(solution)/shard_map/ppermute | solution.py:41
  144.2 6.9 %collective-permute-start.2 = (f32[800,400]{0,1:T(8,128)S(1)}, f32[800,400]{0,1:T(8,128)}, u32[]{:S(2)}, u32[]{:S(2)}) collective-permute-start(f32[800,400]{0,1:T(8,128)S(1)} %collective-permute-done.1), channel_id=1, source_target_pairs={{0,1},{1,0},{2,3},{3,2},{4,5},{5,4},{6,7},{7,6},{8,9},{9,8},{10,11... | collective-permute-start | bytes 3840008 | tf_op jit(solution)/shard_map/ppermute | solution.py:42
Sparse Core Ops, SparseCore 0:
  34.3 116.4 all-gather.1

commit v5 on v4

--- a/solution.py
+++ b/solution.py
@@ -14,9 +14,10 @@
     pair_rows = amplitudes.shape[0]
     b_count = amplitudes.shape[1] // V
     virt_local = V // row_count
-    outgoing = amplitudes.reshape(pair_rows, b_count, V).transpose(2, 1, 0)
-    received = lax.all_to_all(outgoing, ROW, split_axis=0, concat_axis=2, tiled=True)
-    set_rows = received.shape[2] // O
+    outgoing = amplitudes.reshape(pair_rows, b_count, V).transpose(2, 1, 0).reshape(V, b_count * pair_rows)
+    received = lax.all_to_all(outgoing, ROW, split_axis=0, concat_axis=0, tiled=True)
+    received = received.reshape(row_count, virt_local, b_count, pair_rows).transpose(1, 2, 0, 3)
+    set_rows = row_count * pair_rows // O
     blocks = received.reshape(virt_local, b_count, set_rows, O).transpose(0, 2, 1, 3)
     return blocks.reshape(virt_local * set_rows, b_count * O)
 

time: 192 us -> 204 us (1.062)
  blocking collectives: 49.9 us -> 67 us
  other arithmetic: 11.6 us -> 6.47 us
    all_to_all x1, blocking collectives: 49.9 us -> 67 us  [regroup_local(): lax.all_to_all(outgoing, ROW, split_axis=0, concat_axis=0, tiled=True)]
    unnamed x5 -> x3, local copies, waits for them, and re-layouts: 8.36 us -> 1.71 us
    all_to_all x1 -> x0, other arithmetic: 5.13 us -> none  [regroup_local(): lax.all_to_all(outgoing, ROW, split_axis=0, concat_axis=2, tiled=True)]
    reshape x0 -> x1, local copies, waits for them, and re-layouts: none -> 2.7 us  [regroup_local(): received.reshape(row_count, virt_local, b_count, pair_rows)]
    transpose x1 -> x2, local copies, waits for them, and re-layouts: 2.44 us -> 4.12 us  [the longest x1 2.44 us: regroup_local(): amplitudes.reshape(pair_rows, b_count, V).transpose(2, 1, 0)]
  transfers between devices with their start and end apart: 7 -> 7, of which waited for: 4 -> 4; matrix products, arithmetic and copies ran while one was open for 19% -> 14% of each run, Pallas kernels for 0% -> 0%
where the time goes in v5:
time: 204 us; the launch traced here: 202 us
  blocking collectives  67 us (33%)
  waiting for transfers between devices  44.1 us (22%)
  matrix products  28.6 us (14%)
  local copies, waits for them, and re-layouts  25.7 us (13%)
  starting transfers between devices  17.2 us (8%)
  between operations  13.5 us (7%)
  other arithmetic  6.47 us (3%)
    all_to_all x1, blocking collectives, regroup_local(): lax.all_to_all(outgoing, ROW, split_axis=0, concat_axis=0, tiled=True)  67 us
    dot_general x1, matrix products, local(): lax.dot_general(regrouped, part, (((1, 2), (0, 1)), ((), ())), precision=...  28.6 us
    ppermute x1, waiting for transfers between devices, exchange_col(): from_zl = lax.ppermute(block, 'zl', swap)  26.9 us
    ppermute x1, waiting for transfers between devices, ring_zh(): from_right = lax.ppermute(part, 'zh', left)  7.47 us
    ppermute x1, starting transfers between devices, ring_zh(): from_right = lax.ppermute(part, 'zh', left)  6.84 us
    ppermute x1, waiting for transfers between devices, ring_zh(): from_far = lax.ppermute(part, 'zh', across)  6.69 us
    transpose x1, local copies, waits for them, and re-layouts, regroup_local(): received.reshape(virt_local, b_count, set_rows, O).transpose(0, 2, 1, 3)  5.27 us
    reshape x1, local copies, waits for them, and re-layouts, regroup_local(): received.reshape(virt_local, b_count, set_rows, O).transpose(0, 2, 1, 3)  4.74 us
  transfers between devices with their start and end apart: 7, of which 4 were waited for; matrix products, arithmetic and copies ran while one was open for 14% of the time, Pallas kernels for 0%

profile of v5, /device:TPU:1, one launch (start us, length us, event | category | flops | bytes accessed | tf_op | source)
XLA Modules:
  0.0 202.5 jit_solution(890589919702034907)
XLA Ops:
  6.5 0.0 all-gather.2.cloned.1.call-start
  6.5 6.8 %collective-permute-start.3 = (f32[25,2048]{1,0:T(8,128)}, f32[25,2048]{1,0:T(8,128)S(1)}, u32[]{:S(2)}, u32[]{:S(2)}) collective-permute-start(f32[25,2048]{1,0:T(8,128)} %param.3), channel_id=1, source_target_pairs={{0,192},{64,0},{128,64},{192,128},{1,193},{65,1},{129,65},{193,129... | collective-permute-start | bytes 614408 | tf_op jit(solution)/shard_map/ppermute | solution.py:30
  13.4 0.0 collective-permute-start.5
  13.4 3.3 %collective-permute-start.4 = (f32[25,2048]{1,0:T(8,128)}, f32[25,2048]{1,0:T(8,128)S(1)}, u32[]{:S(2)}, u32[]{:S(2)}) collective-permute-start(f32[25,2048]{1,0:T(8,128)} %param.3), channel_id=1, source_target_pairs={{0,128},{64,192},{128,0},{192,64},{1,129},{65,193},{129,1},{193,65... | collective-permute-start | bytes 614408 | tf_op jit(solution)/shard_map/ppermute | solution.py:31
  16.6 1.1 stack.35
  17.8 7.5 %collective-permute-done.3 = f32[25,2048]{1,0:T(8,128)S(1)} collective-permute-done((f32[25,2048]{1,0:T(8,128)}, f32[25,2048]{1,0:T(8,128)S(1)}, u32[]{:S(2)}, u32[]{:S(2)}) %collective-permute-start.3) | collective-permute-done | bytes 204832 | tf_op jit(solution)/shard_map/ppermute | solution.py:30
  25.2 0.1 stack.36
  25.4 0.0 collective-permute-done.5
  25.4 0.1 stack.38
  25.5 0.0 copy-start
  25.5 6.7 %collective-permute-done.4 = f32[25,2048]{1,0:T(8,128)S(1)} collective-permute-done((f32[25,2048]{1,0:T(8,128)}, f32[25,2048]{1,0:T(8,128)S(1)}, u32[]{:S(2)}, u32[]{:S(2)}) %collective-permute-start.4) | collective-permute-done | bytes 204832 | tf_op jit(solution)/shard_map/ppermute | solution.py:31
  32.2 0.1 stack.37
  32.4 1.8 pad_maximum_fusion
  34.2 0.0 all-gather.2.cloned.1.call-update
  34.2 0.0 copy-done
  34.2 1.7 copy.8
  35.9 2.4 %copy.9 = f32[320,10,100]{2,1,0:T(8,128)S(1)} copy(f32[320,10,100]{2,0,1:T(8,128)} %bitcast.23) | data formatting | bytes 2560000 | tf_op jit(solution)/shard_map/transpose | solution.py:17
  38.4 2.0 all_to_all.6
  40.4 67.0 %all_to_all.9 = f32[64,5,1000]{2,1,0:T(8,128)S(1)} all-to-all(f32[64,5,1000]{2,1,0:T(8,128)} %all_to_all.6), channel_id=1, replica_groups=mesh['zh'=4,'y'=4,'x'=4,'zl'=2,'core'=2] {'zh','y','x'}, dimensions={0} | all-to-all | bytes 2560000 | tf_op jit(solution)/shard_map/all_to_all | solution.py:18
  107.4 1.8 copy.10
  109.2 2.7 %reshape.18 = f32[64,5,10,100]{3,2,0,1:T(8,128)S(1)} reshape(f32[64,5,1000]{2,0,1:T(8,128)} %copy.10) | data formatting | bytes 2560000 | tf_op jit(solution)/shard_map/reshape | solution.py:19
  111.9 1.7 copy.11
  113.6 4.7 %reshape.19 = f32[5,10,160,40]{3,2,1,0:T(8,128)} reshape(f32[5,10,64,100]{3,2,1,0:T(8,128)} %copy.11) | data formatting | bytes 2560000 | tf_op jit(solution)/shard_map/reshape | solution.py:21
  118.3 5.3 %copy.12 = f32[5,160,10,40]{1,0,3,2:T(8,128)S(1)} copy(f32[5,160,10,40]{3,1,2,0:T(8,128)} %bitcast.21) | data formatting | bytes 2560000 | tf_op jit(solution)/shard_map/transpose | solution.py:21
  123.6 1.8 reshape.20
  125.4 0.0 collective-permute-start.1
  125.4 3.2 %collective-permute-start = (f32[800,400]{0,1:T(8,128)}, f32[800,400]{0,1:T(8,128)S(1)}, u32[]{:S(2)}, u32[]{:S(2)}) collective-permute-start(f32[800,400]{0,1:T(8,128)} %reshape.20), channel_id=1, source_target_pairs={{0,1},{1,0},{2,3},{3,2},{4,5},{5,4},{6,7},{7,6},{8,9},{9,8},{10,11... | collective-permute-start | bytes 3840008 | tf_op jit(solution)/shard_map/ppermute | solution.py:42
  128.6 26.9 %collective-permute-done.1 = f32[800,400]{0,1:T(8,128)S(1)} collective-permute-done((f32[800,400]{0,1:T(8,128)}, f32[800,400]{0,1:T(8,128)S(1)}, u32[]{:S(2)}, u32[]{:S(2)}) %collective-permute-start.1) | collective-permute-done | bytes 1280032 | tf_op jit(solution)/shard_map/ppermute | solution.py:41
  155.5 3.9 %collective-permute-start.2 = (f32[800,400]{0,1:T(8,128)S(1)}, f32[800,400]{0,1:T(8,128)}, u32[]{:S(2)}, u32[]{:S(2)}) collective-permute-start(f32[800,400]{0,1:T(8,128)S(1)} %collective-permute-done.1), channel_id=1, source_target_pairs={{0,1},{1,0},{2,3},{3,2},{4,5},{5,4},{6,7},{7,6},{8,9},{9,8},{10,11... | collective-permute-start | bytes 3840008 | tf_op jit(solution)/shard_map/ppermute | solution.py:43
  159.4 0.0 collective-permute-done
  159.4 3.0 %collective-permute-done.2 = f32[800,400]{0,1:T(8,128)} collective-permute-done((f32[800,400]{0,1:T(8,128)S(1)}, f32[800,400]{0,1:T(8,128)}, u32[]{:S(2)}, u32[]{:S(2)}) %collective-permute-start.2) | collective-permute-done | bytes 1280032 | tf_op jit(solution)/shard_map/ppermute | solution.py:43
  162.4 4.7 %select_bitcast_fusion.3 = (f32[800,1,400]{0,2,1:T(8,128)}, f32[800,1,400]{0,2,1:T(8,128)}, f32[800,1,400]{0,2,1:T(8,128)}, f32[800,1,400]{0,2,1:T(8,128)}) fusion(f32[800,400]{0,1:T(8,128)} %reshape.20, f32[800,400]{0,1:T(8,128)S(1)} %collective-permute-done, f32[800,400]{0,1:T(8,128)S(1)} %collective-permute-done.1, f32[800,400]{0,1:T(8,128)} %collective-permute-done.2, ...), kind=kLoop, calls=%fused_computation.13 | loop fusion | flops 3840000 | bytes 10240012 | tf_op jit(solution)/shard_map/stack | solution.py:51
  167.1 0.0 all-gather.2.cloned.1.call-done
  167.1 28.6 %fusion.9 = f32[800,2048]{1,0:T(8,128)} fusion(f32[4,400,2048]{2,0,1:T(4,128)} %all-gather.2.cloned.1.call-done, f32[800,1,400]{0,2,1:T(8,128)} %get-tuple-element.6, f32[800,1,400]{0,2,1:T(8,128)} %get-tuple-element.7, f32[800,1,400]{0,2,1:T(8,128)} %get-tuple-element.8, f32[800,1,400]{0,2,1:T(8,128)} %get-tuple-element.5), kind=kOutput, calls=%fused_computation.9 | convolution fusion | flops 15732480000 | bytes 24780800 | tf_op jit(solution)/shard_map/dot_general | solution.py:68
Async XLA Ops:
  6.5 160.5 %all-gather.2.cloned.1.call-start = ((), (), s32[]{:S(2)}) async-start(), calls=%async_computation.1 | async-start | bytes 13926400 | tf_op jit(solution)/shard_map/all_gather | solution.py:66
  6.5 18.7 %collective-permute-start.3 = (f32[25,2048]{1,0:T(8,128)}, f32[25,2048]{1,0:T(8,128)S(1)}, u32[]{:S(2)}, u32[]{:S(2)}) collective-permute-start(f32[25,2048]{1,0:T(8,128)} %param.3), channel_id=1, source_target_pairs={{0,192},{64,0},{128,64},{192,128},{1,193},{65,1},{129,65},{193,129... | collective-permute-start | bytes 614408 | tf_op jit(solution)/shard_map/ppermute | solution.py:30
  13.4 12.0 %collective-permute-start.5 = (f32[25,2048]{1,0:T(8,128)}, f32[25,2048]{1,0:T(8,128)S(1)}, u32[]{:S(2)}, u32[]{:S(2)}) collective-permute-start(f32[25,2048]{1,0:T(8,128)} %param.3), channel_id=1, source_target_pairs={{0,64},{64,128},{128,192},{192,0},{1,65},{65,129},{129,193},{193,1... | collective-permute-start | bytes 614408 | tf_op jit(solution)/shard_map/ppermute | solution.py:29
  13.4 18.9 %collective-permute-start.4 = (f32[25,2048]{1,0:T(8,128)}, f32[25,2048]{1,0:T(8,128)S(1)}, u32[]{:S(2)}, u32[]{:S(2)}) collective-permute-start(f32[25,2048]{1,0:T(8,128)} %param.3), channel_id=1, source_target_pairs={{0,128},{64,192},{128,0},{192,64},{1,129},{65,193},{129,1},{193,65... | collective-permute-start | bytes 614408 | tf_op jit(solution)/shard_map/ppermute | solution.py:31
  25.5 8.7 %copy-start = (f32[100,3200]{1,0:T(8,128)S(1)}, f32[100,3200]{1,0:T(8,128)}, u32[]{:S(2)}) copy-start(f32[100,3200]{1,0:T(8,128)} %param.2) | copy-start | bytes 3840004
  125.4 30.1 %collective-permute-start.1 = (f32[800,400]{0,1:T(8,128)}, f32[800,400]{0,1:T(8,128)S(1)}, u32[]{:S(2)}, u32[]{:S(2)}) collective-permute-start(f32[800,400]{0,1:T(8,128)} %reshape.20), channel_id=1, source_target_pairs={{0,2},{2,0},{1,3},{3,1},{4,6},{6,4},{5,7},{7,5},{8,10},{10,8},{9,1... | collective-permute-start | bytes 3840008 | tf_op jit(solution)/shard_map/ppermute | solution.py:41
  125.4 34.0 %collective-permute-start = (f32[800,400]{0,1:T(8,128)}, f32[800,400]{0,1:T(8,128)S(1)}, u32[]{:S(2)}, u32[]{:S(2)}) collective-permute-start(f32[800,400]{0,1:T(8,128)} %reshape.20), channel_id=1, source_target_pairs={{0,1},{1,0},{2,3},{3,2},{4,5},{5,4},{6,7},{7,6},{8,9},{9,8},{10,11... | collective-permute-start | bytes 3840008 | tf_op jit(solution)/shard_map/ppermute | solution.py:42
  155.5 6.9 %collective-permute-start.2 = (f32[800,400]{0,1:T(8,128)S(1)}, f32[800,400]{0,1:T(8,128)}, u32[]{:S(2)}, u32[]{:S(2)}) collective-permute-start(f32[800,400]{0,1:T(8,128)S(1)} %collective-permute-done.1), channel_id=1, source_target_pairs={{0,1},{1,0},{2,3},{3,2},{4,5},{5,4},{6,7},{7,6},{8,9},{9,8},{10,11... | collective-permute-start | bytes 3840008 | tf_op jit(solution)/shard_map/ppermute | solution.py:43
Sparse Core Ops, SparseCore 0:
  34.3 127.1 all-gather.1
